TPU v7x, 32 devices: a whole 2x2x4 slice. The times are simulated.
32 devices in a mesh: dp: 4 (over y, x), expert: 8 (over z, core).
Axes of the slice: x: 2, y: 2, z: 4, core: 2. Of those that a mesh axis runs over, the one named last changes fastest.
Arguments:
- context: bfloat16 [8, 4, 128, 1536], P('expert', None, None, 'dp'), may hold values from -0.29882812 to 0.29882812
- w_proj: bfloat16 [1536, 1536], P('dp'), may hold values from -0.15625 to 0.15625
- residual: bfloat16 [4096, 1536], P(('dp', 'expert')), may hold values from -0.29882812 to 0.29882812
- gain_first: float32 [1536], replicated, may hold values from 0.25 to 1.75
- gain_next: float32 [1536], replicated, may hold values from 0.25 to 1.75
- w_router: bfloat16 [1536, 40], replicated, may hold values from -0.15625 to 0.15625
- expert_ids: int32 [4096, 8], P(('dp', 'expert')), may hold values from 0 to 39, all different within a row
- replica_pick: int32 [4096, 8], P(('dp', 'expert')), may hold values from 0 to 5039
- slot_expert: int32 [48], replicated, may hold values from 0 to 39, as said below
- cap_blocks: int32 [48], replicated, may hold values from 1 to 4
- w_in: bfloat16 [48, 1536, 1024], P('expert', 'dp'), as said below
- w_out: bfloat16 [48, 512, 1536], P('expert', 'dp'), as said below
Outputs:
- residual_out: bfloat16 [4096, 1536], P(('dp', 'expert'))
- next_normed: bfloat16 [4096, 1536], P(('dp', 'expert'))
Inputs may be any that keep to these rules, and one draw needn't show every extreme that they name: `slot_expert`: every expert is held by at least one slot; slot s lies on index s // 6 of the expert axis. `w_in`: two slots that hold the same expert have equal weights. `w_out`: two slots that hold the same expert have equal weights.
All inputs are finite; a program needn't handle non-finite values.
Results may differ from a plain program's by a relative error of at most 0.01.
Values may be sent and summed in bfloat16 or wider, within the bound.
No kernel may reach another device: no remote copies, remote signals or barrier semaphores. Data moves between devices by JAX's collectives and lax.ppermute only.
A program may use at most 128 MiB of HBM per device.

v0:
```python
import jax
import jax.numpy as jnp
from jax import lax
from jax.sharding import PartitionSpec as P

CAP_UNIT = 8
CAP_MOST = 32


def rms_scale(values, gain):
    widened = values.astype(jnp.float32)
    return widened * lax.rsqrt(jnp.mean(widened * widened, axis=-1, keepdims=True) + 1e-06) * gain


def route_rows(
    normed, w_router, expert_ids, replica_pick, slot_expert, cap_blocks, groups, cap_unit
):
    row_count = normed.shape[0]
    experts_all = w_router.shape[1]
    slots_all = slot_expert.shape[0]
    topk_all = expert_ids.shape[1]
    logits = jnp.dot(normed, w_router, preferred_element_type=jnp.float32)
    expert_axis = jnp.arange(experts_all)
    one_hot = expert_ids[:, :, None] == expert_axis
    chosen = jnp.sum(jnp.where(one_hot, logits[:, None, :], jnp.float32(0.0)), axis=-1)
    raised = jnp.exp(chosen)
    gates = raised / jnp.sum(raised, axis=-1, keepdims=True)
    holder = (slot_expert[None, :] == expert_axis[:, None]).astype(jnp.int32)
    rep_count = jnp.sum(holder, axis=1)
    earlier = jnp.cumsum(holder, axis=1) - holder
    slot_rank = jnp.sum(earlier * holder, axis=0)
    count_of = jnp.sum(jnp.where(one_hot, rep_count, 0), axis=-1)
    replica = replica_pick % count_of
    slot_axis = jnp.arange(slots_all)
    matched = (slot_expert == expert_ids[:, :, None]) & (slot_rank == replica[:, :, None])
    target_slot = jnp.sum(jnp.where(matched, slot_axis, 0), axis=-1)
    selected = matched.astype(jnp.int32).reshape(groups, -1, slots_all)
    before = jnp.cumsum(selected, axis=1) - selected
    position = jnp.sum(before * selected, axis=-1).reshape(row_count, topk_all)
    capacity = (
        jnp.sum(jnp.where(target_slot[:, :, None] == slot_axis, cap_blocks, 0), axis=-1) * cap_unit
    )
    retained = position < capacity
    return (gates, target_slot, position, retained)


def on_device(
    context,
    w_proj,
    residual,
    gain_first,
    gain_next,
    w_router,
    expert_ids,
    replica_pick,
    slot_expert,
    cap_blocks,
    w_in,
    w_out,
):
    tok_rows = residual.shape[0]
    model_width = residual.shape[1]
    topk_all = expert_ids.shape[1]
    slots_all = slot_expert.shape[0]
    slot_local = w_in.shape[0]
    expert_count = lax.axis_size("expert")
    full_in, full_out = (
        lax.all_gather(w_in, "dp", axis=1, tiled=True),
        lax.all_gather(w_out, "dp", axis=1, tiled=True),
    )
    hidden_units = full_in.shape[2] // 2
    flat_context = context.reshape(-1, context.shape[3])
    attended = lax.psum_scatter(
        jnp.dot(flat_context, w_proj, preferred_element_type=jnp.float32),
        "dp",
        scatter_dimension=0,
        tiled=True,
    )
    hidden_state = (residual.astype(jnp.float32) + attended).astype(jnp.bfloat16)
    normed = rms_scale(hidden_state, gain_first).astype(jnp.bfloat16)
    gates, target_slot, position, retained = route_rows(
        normed, w_router, expert_ids, replica_pick, slot_expert, cap_blocks, 1, CAP_UNIT
    )
    target = jnp.where(retained, position, CAP_MOST)
    spread_rows = jnp.broadcast_to(normed[:, None, :], (tok_rows, topk_all, model_width))
    outgoing = (
        jnp.zeros((slots_all, CAP_MOST, model_width), jnp.bfloat16)
        .at[target_slot, target]
        .set(spread_rows, mode="drop")
    )
    received = lax.all_to_all(outgoing, "expert", split_axis=0, concat_axis=0, tiled=True)
    received = received.reshape(expert_count, slot_local, CAP_MOST, model_width)
    gate_up = jnp.einsum("jsrd,sdf->jsrf", received, full_in, preferred_element_type=jnp.float32)
    activated = (jax.nn.silu(gate_up[..., :hidden_units]) * gate_up[..., hidden_units:]).astype(
        jnp.bfloat16
    )
    expert_out = jnp.einsum(
        "jsrf,sfd->jsrd", activated, full_out, preferred_element_type=jnp.float32
    ).astype(jnp.bfloat16)
    expert_out = expert_out.reshape(slots_all, CAP_MOST, model_width)
    returned = lax.all_to_all(expert_out, "expert", split_axis=0, concat_axis=0, tiled=True)
    clipped = jnp.minimum(position, CAP_MOST - 1)
    picked = returned[target_slot, clipped]
    weighting = jnp.where(retained, gates, jnp.float32(0.0))
    combined = jnp.sum(weighting[:, :, None] * picked.astype(jnp.float32), axis=1)
    residual_out = (hidden_state.astype(jnp.float32) + combined).astype(jnp.bfloat16)
    next_normed = rms_scale(residual_out, gain_next).astype(jnp.bfloat16)
    return (residual_out, next_normed)


def solution(mesh):
    placed = (
        P("expert", None, None, "dp"),
        P("dp", None),
        P(("dp", "expert"), None),
        P(),
        P(),
        P(),
        P(("dp", "expert"), None),
        P(("dp", "expert"), None),
        P(),
        P(),
        P("expert", "dp", None),
        P("expert", "dp", None),
    )
    return jax.shard_map(
        on_device,
        mesh=mesh,
        in_specs=placed,
        out_specs=(P(("dp", "expert"), None), P(("dp", "expert"), None)),
        check_vma=False,
    )
```

profile of v0, /device:TPU:0, one launch (start us, length us, event | category | flops | bytes accessed | tf_op | source)
XLA Modules:
  0.0 491.7 jit_solution(5937265904727964733)
XLA Ops:
  7.2 1.2 copy-done
  8.4 3.7 fusion.36
  12.3 0.7 all-gather.3.cloned.1.call-update
  13.1 0.7 all-gather.5.cloned.1.call-update
  13.9 0.2 reduce_window_sum.31
  14.9 13.5 %reduce-window.6 = s32[1,48,8,128]{3,2,1,0:T(8,128)S(1)} reduce-window(s32[1,48,8,128]{3,2,1,0:T(8,128)S(1)} %bitcast.57, s32[]{:T(128)} %constant.11.clone.1), window={size=1x1x1x128 pad=0_0x0_0x0_0x127_0}, to_apply=%region_5.6 | reduce-window | flops 6242304 | bytes 393220 | tf_op jit(solution)/shard_map/reduce-window
  29.2 0.1 select_reduce_fusion.1
  29.9 29.2 %reduce-scatter.2.cloned.1.call-done = f32[128,1536]{1,0:T(8,128)} async-done(((f32[512,1536]{1,0:T(8,128)}), f32[128,1536]{1,0:T(8,128)}) %reduce-scatter.2.cloned.1.call-update) | async-done | bytes 786448 | tf_op jit(solution)/shard_map/reduce_scatter | solution.py:73
  59.1 1.3 fusion.23
  60.4 0.2 fusion.25
  60.6 9.2 %scatter_custom_fusion = bf16[1536,1536]{1,0:T(8,128)(2,1)} fusion(s32[1024]{0:T(1024)S(1)} %reshape.358, bf16[]{:T(256)} %constant.33.clone.1, bf16[128,1536]{1,0:T(8,128)(2,1)S(1)} %fusion.25), kind=kCustom, calls=%fused_computation.12 | custom fusion | bytes 5111810
  69.8 109.9 %all_to_all.10 = bf16[48,32,1536]{2,1,0:T(8,128)(2,1)} all-to-all(bf16[48,32,1536]{2,1,0:T(8,128)(2,1)} %bitcast.54), channel_id=1, replica_groups=mesh['dp'=4,'expert'=8] {'expert'}, dimensions={0} | all-to-all | bytes 9437184 | tf_op jit(solution)/shard_map/all_to_all | solution.py:91
  179.7 56.9 %all-gather.3.cloned.1.call-done = bf16[6,1536,1024]{2,1,0:T(8,128)(2,1)} async-done(((bf16[6,384,1024]{2,1,0:T(8,128)(2,1)}), bf16[6,1536,1024]{2,1,0:T(8,128)(2,1)}) %all-gather.3.cloned.1.call-update) | async-done | bytes 18874384 | tf_op jit(solution)/shard_map/all_gather | solution.py:68
  236.6 12.1 %fusion.11 = f32[8,6,32,1024]{3,2,0,1:T(8,128)} fusion(bf16[6,1536,1024]{2,1,0:T(8,128)(2,1)} %all-gather.3.cloned.1.call-done, bf16[8,6,32,1536]{3,2,1,0:T(8,128)(2,1)} %bitcast.55), kind=kOutput, calls=%fused_computation.14 | convolution fusion | flops 4831838208 | bytes 29884416 | tf_op jit(solution)/shard_map/jsrd,sdf->jsrf/dot_general | solution.py:93
  248.7 86.0 %all-gather.5.cloned.1.call-done = bf16[6,512,1536]{2,1,0:T(8,128)(2,1)} async-done(((bf16[6,128,1536]{2,1,0:T(8,128)(2,1)}), bf16[6,512,1536]{2,1,0:T(8,128)(2,1)}) %all-gather.5.cloned.1.call-update) | async-done | bytes 9437200 | tf_op jit(solution)/shard_map/all_gather | solution.py:69
  334.7 8.2 %convert_bitcast_fusion = bf16[8,6,32,1536]{3,2,0,1:T(8,128)(2,1)S(1)} fusion(bf16[6,512,1536]{2,1,0:T(8,128)(2,1)} %all-gather.5.cloned.1.call-done, f32[8,6,32,1024]{3,2,0,1:T(8,128)} %fusion.11), kind=kOutput, calls=%fused_computation.9 | convolution fusion | flops 2422996992 | bytes 20447232 | tf_op jit(solution)/shard_map/jsrf,sfd->jsrd/dot_general | solution.py:97
  342.9 2.5 copy.63
  345.4 4.9 all-to-all-start.1
  350.6 0.2 fusion.37
  351.1 104.5 %all-to-all-done.1 = bf16[48,32,1536]{2,1,0:T(8,128)(2,1)} async-done(((bf16[48,32,1536]{2,1,0:T(8,128)(2,1)}), bf16[48,32,1536]{2,1,0:T(8,128)(2,1)}, u32[]{:S(2)}, u32[]{:S(2)}) %all-to-all-start.1) | async-done | bytes 4718624 | tf_op jit(solution)/shard_map/all_to_all | solution.py:101
  455.5 23.7 %gather_fusion = bf16[1024,1536]{1,0:T(8,128)(2,1)} fusion(bf16[48,32,1536]{2,1,0:T(8,128)(2,1)} %all-to-all-done.1, s32[1024]{0:T(1024)S(1)} %reshape.352), kind=kCustom, calls=%fused_computation | custom fusion | bytes 6299648 | tf_op jit(solution)/shard_map/gather | solution.py:103
  479.2 4.7 fusion.4
  484.0 0.2 fusion.20
  484.2 0.9 fusion.22
  (67 shorter events, 2.8 us)
Async XLA Ops:
  7.2 1.3 copy-start
  7.2 51.9 %reduce-scatter.2.cloned.1.call-start = ((), (), s32[]{:S(2)}) async-start(), calls=%async_computation.3 | async-start | bytes 3932160 | tf_op jit(solution)/shard_map/reduce_scatter | solution.py:73
  12.2 1.6 copy-start.5
  12.2 1.7 copy-start.6
  12.2 2.1 copy-start.9
  12.2 17.2 %copy-start.10 = (s32[48]{0:T(128)S(1)}, s32[48]{0:T(128)}, u32[]{:S(2)}) copy-start(s32[48]{0:T(128)} %param.21) | copy-start | bytes 580
  12.2 17.3 %copy-start.12 = (s32[2]{0:T(128)S(1)}, s32[2]{0:T(128)}, u32[]{:S(2)}) copy-start(s32[2]{0:T(128)} %constant.41) | copy-start | bytes 28
  12.2 17.4 %copy-start.11 = (s32[2]{0:T(128)S(1)}, s32[2]{0:T(128)}, u32[]{:S(2)}) copy-start(s32[2]{0:T(128)} %constant.44) | copy-start | bytes 28
  12.2 46.9 %copy-start.3 = (bf16[128,1536]{1,0:T(8,128)(2,1)S(1)}, bf16[128,1536]{1,0:T(8,128)(2,1)}, u32[]{:S(2)}) copy-start(bf16[128,1536]{1,0:T(8,128)(2,1)} %param.14) | copy-start | bytes 1179652
  12.2 224.4 %all-gather.3.cloned.1.call-start = ((), (), s32[]{:S(2)}) async-start(), calls=%async_computation.4 | async-start | bytes 23592960 | tf_op jit(solution)/shard_map/all_gather | solution.py:68
  13.0 47.4 %copy-start.7 = (f32[1536]{0:T(1024)S(1)}, f32[1536]{0:T(1024)}, u32[]{:S(2)}) copy-start(f32[1536]{0:T(1024)} %param.15) | copy-start | bytes 18436
  13.0 321.7 %all-gather.5.cloned.1.call-start = ((), (), s32[]{:S(2)}) async-start(), calls=%async_computation.5 | async-start | bytes 11796480 | tf_op jit(solution)/shard_map/all_gather | solution.py:69
  345.4 5.2 %copy-start.4 = (bf16[1536,40]{0,1:T(8,128)(2,1)S(1)}, bf16[1536,40]{0,1:T(8,128)(2,1)}, u32[]{:S(2)}) copy-start(bf16[1536,40]{0,1:T(8,128)(2,1)} %param.17) | copy-start | bytes 368644
  345.4 110.1 %all-to-all-start.1 = ((bf16[48,32,1536]{2,1,0:T(8,128)(2,1)}), bf16[48,32,1536]{2,1,0:T(8,128)(2,1)}, u32[]{:S(2)}, u32[]{:S(2)}) async-start(bf16[48,32,1536]{2,1,0:T(8,128)(2,1)} %bitcast.53), calls=%async_computation.2 | async-start | bytes 9437184 | tf_op jit(solution)/shard_map/all_to_all | solution.py:101
  455.5 29.6 %copy-start.1 = (bf16[384,1536]{1,0:T(8,128)(2,1)S(1)}, bf16[384,1536]{1,0:T(8,128)(2,1)}, u32[]{:S(2)}) copy-start(bf16[384,1536]{1,0:T(8,128)(2,1)} %param.13) | copy-start | bytes 3538948
  479.2 5.0 %copy-start.8 = (f32[1536]{0:T(1024)S(1)}, f32[1536]{0:T(1024)}, u32[]{:S(2)}) copy-start(f32[1536]{0:T(1024)} %param.16) | copy-start | bytes 18436
  484.2 0.9 copy-start.2
Sparse Core Ops, SparseCore 0:
  12.3 46.7 reduce-scatter.1
  60.9 175.6 all-gather.2
  238.5 96.1 all-gather.4
where the time goes:
time: 492 us
  waiting for transfers between devices  278 us (57%)
  blocking collectives  110 us (22%)
  local copies, waits for them, and re-layouts  38.4 us (8%)
  matrix products  24.3 us (5%)
  other arithmetic  22.1 us (4%)
  between operations  14 us (3%)
  starting transfers between devices  5.02 us (1%)
    all_to_all x1, blocking collectives, on_device(): lax.all_to_all(outgoing, 'expert', split_axis=0, concat_axis=0, tiled=True)  110 us
    all_to_all x1, waiting for transfers between devices, on_device(): lax.all_to_all(expert_out, 'expert', split_axis=0, concat_axis=0, tiled=T...  104 us
    all_gather x1, waiting for transfers between devices, on_device(): lax.all_gather(w_out, 'dp', axis=1, tiled=True)  86 us
    all_gather x1, waiting for transfers between devices, on_device(): lax.all_gather(w_in, 'dp', axis=1, tiled=True)  56.9 us
    reduce_scatter x1, waiting for transfers between devices, on_device(): lax.psum_scatter(jnp.dot(flat_context, w_proj, preferred_element_type=jnp...  29.2 us
    gather x1, local copies, waits for them, and re-layouts, on_device(): picked = returned[target_slot, clipped]  23.7 us
    another operation x2, other arithmetic  13.5 us
    dot_general x1, matrix products, on_device(): jnp.einsum('jsrd,sdf->jsrf', received, full_in, preferred_element_type=jn...  12.1 us
  transfers between devices with their start and end apart: 4, of which 4 were waited for; matrix products, arithmetic and copies ran while one was open for 8% of the time, Pallas kernels for 0%

commit v1 on v0

v1 whole, which is shorter than its diff:
```python
import math

import jax
import jax.numpy as jnp
from jax import lax
from jax.sharding import PartitionSpec as P

CAP_UNIT = 8
CAP_MOST = 32


def rms_scale(values, gain):
    widened = values.astype(jnp.float32)
    return widened * lax.rsqrt(jnp.mean(widened * widened, axis=-1, keepdims=True) + 1e-06) * gain


def route_rows(normed, w_router, expert_ids, replica_pick, slot_expert, cap_blocks, cap_unit):
    row_count, topk_all = expert_ids.shape
    experts_all = w_router.shape[1]
    slots_all = slot_expert.shape[0]
    logits = jnp.dot(normed, w_router, preferred_element_type=jnp.float32)
    expert_axis = jnp.arange(experts_all)
    one_hot = expert_ids[:, :, None] == expert_axis
    chosen = jnp.sum(jnp.where(one_hot, logits[:, None, :], jnp.float32(0.0)), axis=-1)
    raised = jnp.exp(chosen)
    gates = raised / jnp.sum(raised, axis=-1, keepdims=True)
    holder = (slot_expert[None, :] == expert_axis[:, None]).astype(jnp.int32)
    rep_count = jnp.sum(holder, axis=1)
    earlier = jnp.cumsum(holder, axis=1) - holder
    slot_rank = jnp.sum(earlier * holder, axis=0)
    count_of = jnp.sum(jnp.where(one_hot, rep_count, 0), axis=-1)
    replica = replica_pick % count_of
    slot_axis = jnp.arange(slots_all)
    matched = (slot_expert == expert_ids[:, :, None]) & (slot_rank == replica[:, :, None])
    target_slot = jnp.sum(jnp.where(matched, slot_axis, 0), axis=-1)
    flat_count = row_count * topk_all
    selected = matched.reshape(flat_count, slots_all)
    flat_axis = lax.optimization_barrier(jnp.arange(flat_count))
    lower = (flat_axis[:, None] > flat_axis[None, :]).astype(jnp.bfloat16)
    before = jnp.dot(lower, selected.astype(jnp.bfloat16), preferred_element_type=jnp.float32)
    position = (
        jnp.sum(jnp.where(selected, before, jnp.float32(0.0)), axis=-1)
        .astype(jnp.int32)
        .reshape(row_count, topk_all)
    )
    capacity = (
        jnp.sum(jnp.where(target_slot[:, :, None] == slot_axis, cap_blocks, 0), axis=-1) * cap_unit
    )
    retained = position < capacity
    return (gates, target_slot, position, retained)


def unit_plan(slot_local, n_dp, hidden_units):
    chunks = n_dp // math.gcd(slot_local, n_dp)
    units_per = slot_local * chunks // n_dp
    chunk_width = hidden_units // chunks
    owned = [[((o * units_per + i) // chunks, (o * units_per + i) % chunks) for i in range(units_per)]
             for o in range(n_dp)]
    first_slot = [owned[o][0][0] for o in range(n_dp)]
    slots_per = max(owned[o][-1][0] - first_slot[o] + 1 for o in range(n_dp))
    return chunks, units_per, chunk_width, owned, first_slot, slots_per


def on_device(
    context,
    w_proj,
    residual,
    gain_first,
    gain_next,
    w_router,
    expert_ids,
    replica_pick,
    slot_expert,
    cap_blocks,
    w_in,
    w_out,
):
    tok_rows, model_width = residual.shape
    topk_all = expert_ids.shape[1]
    slot_local, d_local, _ = w_in.shape
    hidden_units = w_in.shape[2] // 2
    ff_local = w_out.shape[1]
    n_dp = lax.axis_size("dp")
    n_exp = lax.axis_size("expert")
    dp_at = lax.axis_index("dp")
    exp_at = lax.axis_index("expert")
    chunks, units_per, chunk_width, owned, first_slot, slots_per = unit_plan(
        slot_local, n_dp, hidden_units
    )
    sources_per_chunk = chunk_width // ff_local
    slot_rows = n_exp * CAP_MOST
    hub_rows = slot_local * slot_rows

    win_parts, wout_parts = [], []
    for o in range(n_dp):
        win_units, wout_units = [], []
        for s, c in owned[o]:
            lo = c * chunk_width
            win_units.append(
                jnp.concatenate(
                    [w_in[s, :, lo:lo + chunk_width],
                     w_in[s, :, hidden_units + lo:hidden_units + lo + chunk_width]],
                    axis=-1,
                )
            )
            wout_units.append(w_out[s])
        win_parts.append(jnp.stack(win_units))
        wout_parts.append(jnp.stack(wout_units))
    win_recv = lax.all_to_all(jnp.stack(win_parts), "dp", 0, 0, tiled=True)
    wout_recv = lax.all_to_all(jnp.stack(wout_parts), "dp", 0, 0, tiled=True)
    unit_in = win_recv.transpose(1, 0, 2, 3).reshape(units_per, n_dp * d_local, 2 * chunk_width)

    flat_context = context.reshape(-1, context.shape[3])
    attended = lax.psum_scatter(
        jnp.dot(flat_context, w_proj, preferred_element_type=jnp.float32),
        "dp",
        scatter_dimension=0,
        tiled=True,
    )
    hidden_state = (residual.astype(jnp.float32) + attended).astype(jnp.bfloat16)
    normed = rms_scale(hidden_state, gain_first).astype(jnp.bfloat16)
    gates, target_slot, position, retained = route_rows(
        normed, w_router, expert_ids, replica_pick, slot_expert, cap_blocks, CAP_UNIT
    )
    dest = target_slot // slot_local
    row_in_hub = (target_slot % slot_local) * slot_rows + exp_at * CAP_MOST + position
    code = jnp.where(retained, dest * hub_rows + row_in_hub, -1).astype(jnp.int32)
    kept_gates = jnp.where(retained, gates, jnp.float32(0.0))

    normed_all = lax.all_gather(normed, "expert", axis=0, tiled=True)
    code_all = lax.all_gather(code, "expert", axis=0, tiled=True)
    gates_all = lax.all_gather(kept_gates, "expert", axis=0, tiled=True)
    local = code_all - exp_at * hub_rows
    valid = (code_all >= 0) & (local >= 0) & (local < hub_rows)
    local = jnp.where(valid, local, -1)
    hit = local[:, :, None] == jnp.arange(hub_rows)
    pick = jnp.any(hit, axis=1).astype(jnp.bfloat16)
    weight = jnp.sum(jnp.where(hit, gates_all[:, :, None], jnp.float32(0.0)), axis=1)
    slot_in = lax.dot_general(
        pick, normed_all, (((0,), (0,)), ((), ())), preferred_element_type=jnp.float32
    ).astype(jnp.bfloat16)
    slot_in = slot_in.reshape(slot_local, slot_rows, model_width)

    x_parts = []
    for o in range(n_dp):
        x_parts.append(
            jnp.stack([slot_in[min(first_slot[o] + j, slot_local - 1)] for j in range(slots_per)])
        )
    x_recv = lax.all_to_all(jnp.stack(x_parts), "dp", 0, 0, tiled=True)

    unit_rows = n_dp * slot_rows
    y_acc = jnp.zeros((slots_per, unit_rows, model_width), jnp.float32)
    my_first = (dp_at * units_per) // chunks
    for i in range(units_per):
        unit = dp_at * units_per + i
        slot_at = unit // chunks - my_first
        chunk_at = unit % chunks
        rows = lax.dynamic_index_in_dim(x_recv, slot_at, axis=1, keepdims=False)
        rows = rows.reshape(unit_rows, model_width)
        w_down = lax.dynamic_slice_in_dim(
            wout_recv[:, i], chunk_at * sources_per_chunk, sources_per_chunk, axis=0
        ).reshape(chunk_width, model_width)
        gate_up = jnp.dot(rows, unit_in[i], preferred_element_type=jnp.float32)
        activated = (
            jax.nn.silu(gate_up[:, :chunk_width]) * gate_up[:, chunk_width:]
        ).astype(jnp.bfloat16)
        out = jnp.dot(activated, w_down, preferred_element_type=jnp.float32)
        prev = lax.dynamic_index_in_dim(y_acc, slot_at, axis=0, keepdims=False)
        y_acc = lax.dynamic_update_index_in_dim(y_acc, prev + out, slot_at, axis=0)

    y_send = (
        y_acc.reshape(slots_per, n_dp, slot_rows, model_width)
        .transpose(1, 0, 2, 3)
        .astype(jnp.bfloat16)
    )
    y_recv = lax.all_to_all(y_send, "dp", 0, 0, tiled=True)
    slot_out = [None] * slot_local
    for o in range(n_dp):
        mine = {s for s, _ in owned[o]}
        for j in range(slots_per):
            s = first_slot[o] + j
            if s < slot_local and s in mine:
                part = y_recv[o, j].astype(jnp.float32)
                slot_out[s] = part if slot_out[s] is None else slot_out[s] + part
    expert_out = jnp.concatenate(slot_out, axis=0).astype(jnp.bfloat16)

    weight_hi = weight.astype(jnp.bfloat16)
    weight_lo = (weight - weight_hi.astype(jnp.float32)).astype(jnp.bfloat16)
    partial = jnp.dot(weight_hi, expert_out, preferred_element_type=jnp.float32) + jnp.dot(
        weight_lo, expert_out, preferred_element_type=jnp.float32
    )
    combined = lax.psum_scatter(partial, "expert", scatter_dimension=0, tiled=True)
    residual_out = (hidden_state.astype(jnp.float32) + combined).astype(jnp.bfloat16)
    next_normed = rms_scale(residual_out, gain_next).astype(jnp.bfloat16)
    return (residual_out, next_normed)


def solution(mesh):
    placed = (
        P("expert", None, None, "dp"),
        P("dp", None),
        P(("dp", "expert"), None),
        P(),
        P(),
        P(),
        P(("dp", "expert"), None),
        P(("dp", "expert"), None),
        P(),
        P(),
        P("expert", "dp", None),
        P("expert", "dp", None),
    )
    return jax.shard_map(
        on_device,
        mesh=mesh,
        in_specs=placed,
        out_specs=(P(("dp", "expert"), None), P(("dp", "expert"), None)),
        check_vma=False,
    )
```

time: 492 us -> 475 us (0.965)
  blocking collectives: 110 us -> 29 us
  other arithmetic: 22.1 us -> 71.4 us
  waiting for transfers between devices: 278 us -> 258 us
  matrix products: 24.3 us -> 40.7 us
  starting transfers between devices: 5.02 us -> 21.2 us
    all_gather x2 -> x1, waiting for transfers between devices: 143 us -> 0.02 us  [on_device(): normed_all = lax.all_gather(normed, 'expert', axis=0, tiled=True)]
    all_to_all x1 -> x0, blocking collectives: 110 us -> none  [on_device(): lax.all_to_all(outgoing, 'expert', split_axis=0, concat_axis=0, tiled=True)]
    reduce_scatter x0 -> x1, waiting for transfers between devices: none -> 69.9 us  [on_device(): lax.psum_scatter(partial, 'expert', scatter_dimension=0, tiled=True)]
    all_to_all x1 -> x4, waiting for transfers between devices: 104 us -> 147 us  [the longest x1 61.6 us: on_device(): x_recv = lax.all_to_all(jnp.stack(x_parts), 'dp', 0, 0, tiled=True)]
    all_gather x0 -> x2, blocking collectives: none -> 29 us  [the longest x1 14.6 us: on_device(): code_all = lax.all_gather(code, 'expert', axis=0, tiled=True)]
    reduce_or x0 -> x1, other arithmetic: none -> 23.7 us  [on_device(): pick = jnp.any(hit, axis=1).astype(jnp.bfloat16)]
    gather x1 -> x0, local copies, waits for them, and re-layouts: 23.7 us -> none  [on_device(): picked = returned[target_slot, clipped]]
    dot_general x2 -> x10, matrix products: 20.3 us -> 36.9 us  [the longest x3 8.54 us: on_device(): out = jnp.dot(activated, w_down, preferred_element_type=jnp.float32)]
  transfers between devices with their start and end apart: 4 -> 7, of which waited for: 4 -> 6; matrix products, arithmetic and copies ran while one was open for 8% -> 16% of each run, Pallas kernels for 0% -> 0%
where the time goes in v1:
time: 475 us; the launch traced here: 474 us
  waiting for transfers between devices  258 us (54%)
  other arithmetic  71.4 us (15%)
  matrix products  40.7 us (9%)
  local copies, waits for them, and re-layouts  39.7 us (8%)
  blocking collectives  29 us (6%)
  starting transfers between devices  21.2 us (4%)
  between operations  14.3 us (3%)
    reduce_scatter x1, waiting for transfers between devices, on_device(): lax.psum_scatter(partial, 'expert', scatter_dimension=0, tiled=True)  69.9 us
    all_to_all x1, waiting for transfers between devices, on_device(): x_recv = lax.all_to_all(jnp.stack(x_parts), 'dp', 0, 0, tiled=True)  61.6 us
    reduce_scatter x1, waiting for transfers between devices, on_device(): lax.psum_scatter(jnp.dot(flat_context, w_proj, preferred_element_type=jnp...  40.8 us
    all_to_all x1, waiting for transfers between devices, on_device(): y_recv = lax.all_to_all(y_send, 'dp', 0, 0, tiled=True)  35.9 us
    all_to_all x1, waiting for transfers between devices, on_device(): win_recv = lax.all_to_all(jnp.stack(win_parts), 'dp', 0, 0, tiled=True)  32.3 us
    reduce_or x1, other arithmetic, on_device(): pick = jnp.any(hit, axis=1).astype(jnp.bfloat16)  23.7 us
    reduce_sum x1, other arithmetic, on_device(): jnp.sum(jnp.where(hit, gates_all[:, :, None], jnp.float32(0.0)), axis=1)  18.8 us
    all_to_all x1, waiting for transfers between devices, on_device(): wout_recv = lax.all_to_all(jnp.stack(wout_parts), 'dp', 0, 0, tiled=True)  16.9 us
  transfers between devices with their start and end apart: 7, of which 6 were waited for; matrix products, arithmetic and copies ran while one was open for 16% of the time, Pallas kernels for 0%

profile of v1, /device:TPU:0, one launch (start us, length us, event | category | flops | bytes accessed | tf_op | source)
XLA Modules:
  0.0 473.8 jit_solution(8478582062550147527)
XLA Ops:
  18.0 40.8 %reduce-scatter.3.cloned.1.call-done = f32[128,1536]{1,0:T(8,128)} async-done(((f32[512,1536]{1,0:T(8,128)}), f32[128,1536]{1,0:T(8,128)}) %reduce-scatter.3.cloned.1.call-update) | async-done | bytes 786448 | tf_op jit(solution)/shard_map/reduce_scatter | solution.py:114
  65.5 5.2 %all-to-all-start.1 = ((bf16[4,3,384,512]{3,2,1,0:T(8,128)(2,1)}), bf16[4,3,384,512]{3,2,1,0:T(8,128)(2,1)}, u32[]{:S(2)}, u32[]{:S(2)}) async-start(bf16[4,3,384,512]{3,2,1,0:T(8,128)(2,1)} %pad_maximum_fusion.1), calls=%async_computation.2 | async-start | bytes 9437184 | tf_op jit(solution)/shard_map/all_to_all | solution.py:109
  76.7 14.6 %all_gather.9 = s32[1024,8]{0,1:T(8,128)S(1)} all-gather(s32[128,8]{0,1:T(8,128)S(1)} %fusion.49), channel_id=1, replica_groups=mesh['dp'=4,'expert'=8] {'expert'}, dimensions={0}, use_global_device_ids=true | all-gather | bytes 36864 | tf_op jit(solution)/shard_map/all_gather | solution.py:131
  91.5 32.3 %all-to-all-done.1 = bf16[4,3,384,512]{3,2,1,0:T(8,128)(2,1)} async-done(((bf16[4,3,384,512]{3,2,1,0:T(8,128)(2,1)}), bf16[4,3,384,512]{3,2,1,0:T(8,128)(2,1)}, u32[]{:S(2)}, u32[]{:S(2)}) %all-to-all-start.1) | async-done | bytes 4718624 | tf_op jit(solution)/shard_map/all_to_all | solution.py:109
  123.7 5.1 %all-to-all-start.2 = ((bf16[4,3,128,1536]{3,2,1,0:T(8,128)(2,1)}), bf16[4,3,128,1536]{3,2,1,0:T(8,128)(2,1)}, u32[]{:S(2)}, u32[]{:S(2)}) async-start(bf16[4,3,128,1536]{3,2,1,0:T(8,128)(2,1)} %pad_maximum_fusion.2), calls=%async_computation.3 | async-start | bytes 9437184 | tf_op jit(solution)/shard_map/all_to_all | solution.py:110
  128.9 23.7 %fusion = pred[1024,1536]{1,0:T(8,128)(4,1)S(1)} fusion(s32[1024,8]{1,0:T(8,128)S(1)} %copy.50), kind=kLoop, calls=%fused_computation.2 | loop fusion | flops 23592960 | bytes 1605632 | tf_op jit(solution)/shard_map/reduce_or | solution.py:137
  152.6 7.3 %convolution_convert_fusion = bf16[1536,1536]{1,0:T(8,128)(2,1)S(1)} fusion(pred[1024,1536]{1,0:T(8,128)(4,1)S(1)} %fusion, bf16[1024,1536]{1,0:T(8,128)(2,1)} %all-gather.2.cloned.1.call-done), kind=kOutput, calls=%fused_computation.3 | convolution fusion | flops 4834197504 | bytes 9437184 | tf_op jit(solution)/shard_map/dot_general | solution.py:139
  164.3 16.9 %all-to-all-done.2 = bf16[4,3,128,1536]{3,2,1,0:T(8,128)(2,1)} async-done(((bf16[4,3,128,1536]{3,2,1,0:T(8,128)(2,1)}), bf16[4,3,128,1536]{3,2,1,0:T(8,128)(2,1)}, u32[]{:S(2)}, u32[]{:S(2)}) %all-to-all-start.2) | async-done | bytes 4718624 | tf_op jit(solution)/shard_map/all_to_all | solution.py:110
  181.2 5.5 %all-to-all-start = ((bf16[4,2,256,1536]{3,2,1,0:T(8,128)(2,1)}), bf16[4,2,256,1536]{3,2,1,0:T(8,128)(2,1)}, u32[]{:S(2)}, u32[]{:S(2)}) async-start(bf16[4,2,256,1536]{3,2,1,0:T(8,128)(2,1)} %pad_maximum_fusion), calls=%async_computation.1 | async-start | bytes 12582912 | tf_op jit(solution)/shard_map/all_to_all | solution.py:149
  189.6 4.6 fusion.58
  194.3 61.6 %all-to-all-done = bf16[4,2,256,1536]{3,2,1,0:T(8,128)(2,1)} async-done(((bf16[4,2,256,1536]{3,2,1,0:T(8,128)(2,1)}), bf16[4,2,256,1536]{3,2,1,0:T(8,128)(2,1)}, u32[]{:S(2)}, u32[]{:S(2)}) %all-to-all-start) | async-done | bytes 6291488 | tf_op jit(solution)/shard_map/all_to_all | solution.py:149
  255.9 4.5 constant_dynamic-slice_fusion
  260.4 4.6 fusion.65
  267.8 5.8 %dynamic_update_slice.10 = f32[2,1024,1536]{2,1,0:T(8,128)} pad(f32[1,1024,1536]{2,1,0:T(8,128)S(1)} %convolution_bitcast_fusion, f32[]{:T(128)} %constant.128.clone.1), padding=0_1x0_0x0_0 | pad | bytes 18874372 | tf_op jit(solution)/shard_map/jit(dynamic_update_index_in_dim)/dynamic_update_slice | solution.py:169
  273.6 3.8 bitcast_dynamic-update-slice_fusion.1
  286.3 7.9 %convert_element_type.110 = bf16[2,1024,1536]{2,1,0:T(8,128)(2,1)} convert(f32[2,1024,1536]{2,1,0:T(8,128)} %bitcast_dynamic-update-slice_fusion) | non-fusion elementwise | flops 3145728 | bytes 18874368 | tf_op jit(solution)/shard_map/convert_element_type | solution.py:174
  294.2 5.8 %copy.54 = bf16[2,4,256,1536]{3,2,0,1:T(8,128)(2,1)} copy(bf16[2,4,256,1536]{3,2,1,0:T(8,128)(2,1)} %bitcast.179) | data formatting | bytes 12582912 | tf_op jit(solution)/shard_map/convert_element_type | solution.py:174
  300.1 5.2 %all-to-all-start.3 = ((bf16[4,2,256,1536]{3,2,1,0:T(8,128)(2,1)}), bf16[4,2,256,1536]{3,2,1,0:T(8,128)(2,1)}, u32[]{:S(2)}, u32[]{:S(2)}) async-start(bf16[4,2,256,1536]{3,2,1,0:T(8,128)(2,1)} %bitcast.178), calls=%async_computation.4 | async-start | bytes 12582912 | tf_op jit(solution)/shard_map/all_to_all | solution.py:176
  305.4 14.4 %all_gather.10 = f32[1024,8]{0,1:T(8,128)S(1)} all-gather(f32[128,8]{0,1:T(8,128)S(1)} %get-tuple-element.6), channel_id=1, replica_groups=mesh['dp'=4,'expert'=8] {'expert'}, dimensions={0}, use_global_device_ids=true | all-gather | bytes 36864 | tf_op jit(solution)/shard_map/all_gather | solution.py:132
  320.0 18.8 %select_reduce_fusion = f32[1024,1536]{1,0:T(8,128)} fusion(f32[1024,8]{1,0:T(8,128)S(1)} %copy.51, s32[1024,8]{1,0:T(8,128)S(1)} %copy.50), kind=kLoop, calls=%fused_computation | loop fusion | flops 36175872 | bytes 6356992 | tf_op jit(solution)/shard_map/reduce_sum | solution.py:138
  338.8 35.9 %all-to-all-done.3 = bf16[4,2,256,1536]{3,2,1,0:T(8,128)(2,1)} async-done(((bf16[4,2,256,1536]{3,2,1,0:T(8,128)(2,1)}), bf16[4,2,256,1536]{3,2,1,0:T(8,128)(2,1)}, u32[]{:S(2)}, u32[]{:S(2)}) %all-to-all-start.3) | async-done | bytes 6291488 | tf_op jit(solution)/shard_map/all_to_all | solution.py:176
  383.0 5.0 %fusion.6 = f32[1024,1536]{1,0:T(8,128)S(1)} fusion(bf16[1536,1536]{1,0:T(8,128)(2,1)S(1)} %fusion.28, f32[1024,1536]{1,0:T(8,128)S(1)} %copy-done.3), kind=kOutput, calls=%fused_computation.27 | convolution fusion | flops 4833411072 | bytes 17301504 | tf_op jit(solution)/shard_map/dot_general | solution.py:189
  388.1 7.0 %convolution_add_fusion = f32[1024,1536]{1,0:T(8,128)} fusion(f32[1024,1536]{1,0:T(8,128)S(1)} %fusion.6, bf16[1536,1536]{1,0:T(8,128)(2,1)S(1)} %fusion.28, f32[1024,1536]{1,0:T(8,128)S(1)} %copy-done.3), kind=kOutput, calls=%fused_computation.14 | convolution fusion | flops 4839702528 | bytes 23592960 | tf_op jit(solution)/shard_map/dot_general | solution.py:189
  395.1 69.9 %reduce-scatter.5.cloned.1.call-done = f32[128,1536]{1,0:T(8,128)} async-done(((f32[1024,1536]{1,0:T(8,128)}), f32[128,1536]{1,0:T(8,128)}) %reduce-scatter.5.cloned.1.call-update) | async-done | bytes 786448 | tf_op jit(solution)/shard_map/reduce_scatter | solution.py:192
  (110 shorter events, 53.1 us)
Async XLA Ops:
  7.2 1.3 copy-start
  7.2 51.7 %reduce-scatter.3.cloned.1.call-start = ((), (), s32[]{:S(2)}) async-start(), calls=%async_computation.6 | async-start | bytes 3932160 | tf_op jit(solution)/shard_map/reduce_scatter | solution.py:114
  12.1 140.6 %all-gather.2.cloned.1.call-start = ((), (), s32[]{:S(2)}) async-start(), calls=%async_computation.7 | async-start | bytes 3538944 | tf_op jit(solution)/shard_map/all_gather | solution.py:130
  16.7 44.4 %copy-start.13 = (f32[1536]{0:T(1024)S(1)}, f32[1536]{0:T(1024)}, u32[]{:S(2)}) copy-start(f32[1536]{0:T(1024)} %param.15) | copy-start | bytes 18436
  65.4 5.2 %copy-start.12 = (s32[128,8]{0,1:T(8,128)S(1)}, s32[128,8]{0,1:T(8,128)}, u32[]{:S(2)}) copy-start(s32[128,8]{0,1:T(8,128)} %param.18) | copy-start | bytes 12292
  65.4 5.3 %copy-start.15 = (s32[48]{0:T(128)S(1)}, s32[48]{0:T(128)}, u32[]{:S(2)}) copy-start(s32[48]{0:T(128)} %param.20) | copy-start | bytes 580
  65.4 5.8 %copy-start.16 = (s32[128,8]{0,1:T(8,128)S(1)}, s32[128,8]{0,1:T(8,128)}, u32[]{:S(2)}) copy-start(s32[128,8]{0,1:T(8,128)} %param.19) | copy-start | bytes 12292
  65.4 7.4 %copy-start.17 = (s32[48]{0:T(128)S(1)}, s32[48]{0:T(128)}, u32[]{:S(2)}) copy-start(s32[48]{0:T(128)} %param.21) | copy-start | bytes 580
  65.4 7.5 %copy-start.2 = (bf16[6,128,1536]{2,1,0:T(8,128)(2,1)S(1)}, bf16[6,128,1536]{2,1,0:T(8,128)(2,1)}, u32[]{:S(2)}) copy-start(bf16[6,128,1536]{2,1,0:T(8,128)(2,1)} %param.23) | copy-start | bytes 7077892
  65.5 58.3 %all-to-all-start.1 = ((bf16[4,3,384,512]{3,2,1,0:T(8,128)(2,1)}), bf16[4,3,384,512]{3,2,1,0:T(8,128)(2,1)}, u32[]{:S(2)}, u32[]{:S(2)}) async-start(bf16[4,3,384,512]{3,2,1,0:T(8,128)(2,1)} %pad_maximum_fusion.1), calls=%async_computation.2 | async-start | bytes 9437184 | tf_op jit(solution)/shard_map/all_to_all | solution.py:109
  73.8 2.6 copy-start.4
  73.8 2.5 copy-start.11
  123.7 57.5 %all-to-all-start.2 = ((bf16[4,3,128,1536]{3,2,1,0:T(8,128)(2,1)}), bf16[4,3,128,1536]{3,2,1,0:T(8,128)(2,1)}, u32[]{:S(2)}, u32[]{:S(2)}) async-start(bf16[4,3,128,1536]{3,2,1,0:T(8,128)(2,1)} %pad_maximum_fusion.2), calls=%async_computation.3 | async-start | bytes 9437184 | tf_op jit(solution)/shard_map/all_to_all | solution.py:110
  181.2 74.6 %all-to-all-start = ((bf16[4,2,256,1536]{3,2,1,0:T(8,128)(2,1)}), bf16[4,2,256,1536]{3,2,1,0:T(8,128)(2,1)}, u32[]{:S(2)}, u32[]{:S(2)}) async-start(bf16[4,2,256,1536]{3,2,1,0:T(8,128)(2,1)} %pad_maximum_fusion), calls=%async_computation.1 | async-start | bytes 12582912 | tf_op jit(solution)/shard_map/all_to_all | solution.py:149
  260.3 4.6 copy-start.8
  267.8 5.8 %copy-start.10 = (f32[1024,512]{1,0:T(8,128)S(1)}, f32[1024,512]{1,0:T(8,128)}, u32[]{:S(2)}) copy-start(f32[1024,512]{1,0:T(8,128)} %fusion.65) | copy-start | bytes 6291460
  277.4 3.4 copy-start.7
  300.1 74.6 %all-to-all-start.3 = ((bf16[4,2,256,1536]{3,2,1,0:T(8,128)(2,1)}), bf16[4,2,256,1536]{3,2,1,0:T(8,128)(2,1)}, u32[]{:S(2)}, u32[]{:S(2)}) async-start(bf16[4,2,256,1536]{3,2,1,0:T(8,128)(2,1)} %bitcast.178), calls=%async_computation.4 | async-start | bytes 12582912 | tf_op jit(solution)/shard_map/all_to_all | solution.py:176
  305.3 159.7 %reduce-scatter.5.cloned.1.call-start = ((), (), s32[]{:S(2)}) async-start(), calls=%async_computation.8 | async-start | bytes 7077888 | tf_op jit(solution)/shard_map/reduce_scatter | solution.py:192
  377.4 5.6 %copy-start.3 = (f32[1024,1536]{1,0:T(8,128)S(1)}, f32[1024,1536]{1,0:T(8,128)}, u32[]{:S(2)}) copy-start(f32[1024,1536]{1,0:T(8,128)} %select_reduce_fusion) | copy-start | bytes 18874372
  395.0 72.2 %copy-start.1 = (bf16[384,1536]{1,0:T(8,128)(2,1)S(1)}, bf16[384,1536]{1,0:T(8,128)(2,1)}, u32[]{:S(2)}) copy-start(bf16[384,1536]{1,0:T(8,128)(2,1)} %param.13) | copy-start | bytes 3538948
  395.0 69.9 %copy-start.6 = (bf16[128,1536]{1,0:T(8,128)(2,1)S(1)}, bf16[128,1536]{1,0:T(8,128)(2,1)}, u32[]{:S(2)}) copy-start(bf16[128,1536]{1,0:T(8,128)(2,1)} %copy-done.5) | copy-start | bytes 1179652
  395.0 71.3 %copy-start.14 = (f32[1536]{0:T(1024)S(1)}, f32[1536]{0:T(1024)}, u32[]{:S(2)}) copy-start(f32[1536]{0:T(1024)} %param.16) | copy-start | bytes 18436
  466.3 0.9 copy-start.9
  (1 other events, 0.7 us)
Sparse Core Ops, SparseCore 0:
  12.2 46.6 reduce-scatter.2
  62.1 38.4 all-gather.1
  395.2 69.7 reduce-scatter.4

commit v2 on v1

--- a/solution.py
+++ b/solution.py
@@ -15,13 +15,14 @@
 
 
 def route_rows(normed, w_router, expert_ids, replica_pick, slot_expert, cap_blocks, cap_unit):
-    row_count, topk_all = expert_ids.shape
+    blocks, row_count, topk_all = expert_ids.shape
     experts_all = w_router.shape[1]
     slots_all = slot_expert.shape[0]
     logits = jnp.dot(normed, w_router, preferred_element_type=jnp.float32)
+    logits = logits.reshape(blocks, row_count, experts_all)
     expert_axis = jnp.arange(experts_all)
-    one_hot = expert_ids[:, :, None] == expert_axis
-    chosen = jnp.sum(jnp.where(one_hot, logits[:, None, :], jnp.float32(0.0)), axis=-1)
+    one_hot = expert_ids[..., None] == expert_axis
+    chosen = jnp.sum(jnp.where(one_hot, logits[:, :, None, :], jnp.float32(0.0)), axis=-1)
     raised = jnp.exp(chosen)
     gates = raised / jnp.sum(raised, axis=-1, keepdims=True)
     holder = (slot_expert[None, :] == expert_axis[:, None]).astype(jnp.int32)
@@ -31,20 +32,22 @@
     count_of = jnp.sum(jnp.where(one_hot, rep_count, 0), axis=-1)
     replica = replica_pick % count_of
     slot_axis = jnp.arange(slots_all)
-    matched = (slot_expert == expert_ids[:, :, None]) & (slot_rank == replica[:, :, None])
+    matched = (slot_expert == expert_ids[..., None]) & (slot_rank == replica[..., None])
     target_slot = jnp.sum(jnp.where(matched, slot_axis, 0), axis=-1)
     flat_count = row_count * topk_all
-    selected = matched.reshape(flat_count, slots_all)
+    selected = matched.reshape(blocks, flat_count, slots_all)
     flat_axis = lax.optimization_barrier(jnp.arange(flat_count))
     lower = (flat_axis[:, None] > flat_axis[None, :]).astype(jnp.bfloat16)
-    before = jnp.dot(lower, selected.astype(jnp.bfloat16), preferred_element_type=jnp.float32)
+    before = jnp.einsum(
+        "ij,bjs->bis", lower, selected.astype(jnp.bfloat16), preferred_element_type=jnp.float32
+    )
     position = (
         jnp.sum(jnp.where(selected, before, jnp.float32(0.0)), axis=-1)
         .astype(jnp.int32)
-        .reshape(row_count, topk_all)
+        .reshape(blocks, row_count, topk_all)
     )
     capacity = (
-        jnp.sum(jnp.where(target_slot[:, :, None] == slot_axis, cap_blocks, 0), axis=-1) * cap_unit
+        jnp.sum(jnp.where(target_slot[..., None] == slot_axis, cap_blocks, 0), axis=-1) * cap_unit
     )
     retained = position < capacity
     return (gates, target_slot, position, retained)
@@ -88,8 +91,6 @@
         slot_local, n_dp, hidden_units
     )
     sources_per_chunk = chunk_width // ff_local
-    slot_rows = n_exp * CAP_MOST
-    hub_rows = slot_local * slot_rows
 
     win_parts, wout_parts = [], []
     for o in range(n_dp):
@@ -106,49 +107,64 @@
             wout_units.append(w_out[s])
         win_parts.append(jnp.stack(win_units))
         wout_parts.append(jnp.stack(wout_units))
-    win_recv = lax.all_to_all(jnp.stack(win_parts), "dp", 0, 0, tiled=True)
-    wout_recv = lax.all_to_all(jnp.stack(wout_parts), "dp", 0, 0, tiled=True)
+    win_send = jnp.stack(win_parts)
+    wout_send = jnp.stack(wout_parts)
+    both_recv = lax.all_to_all(
+        jnp.stack([win_send, wout_send.reshape(win_send.shape)], axis=2), "dp", 0, 0, tiled=True
+    )
+    win_recv = both_recv[:, :, 0]
+    wout_recv = both_recv[:, :, 1].reshape(wout_send.shape)
     unit_in = win_recv.transpose(1, 0, 2, 3).reshape(units_per, n_dp * d_local, 2 * chunk_width)
+
+    ids_all = lax.all_gather(
+        jnp.concatenate([expert_ids, replica_pick], axis=1), "expert", axis=0, tiled=True
+    ).reshape(n_exp, tok_rows, 2 * topk_all)
 
     flat_context = context.reshape(-1, context.shape[3])
     attended = lax.psum_scatter(
-        jnp.dot(flat_context, w_proj, preferred_element_type=jnp.float32),
+        jnp.dot(flat_context, w_proj, preferred_element_type=jnp.float32).astype(jnp.bfloat16),
         "dp",
         scatter_dimension=0,
         tiled=True,
     )
-    hidden_state = (residual.astype(jnp.float32) + attended).astype(jnp.bfloat16)
+    hidden_state = (residual.astype(jnp.float32) + attended.astype(jnp.float32)).astype(
+        jnp.bfloat16
+    )
     normed = rms_scale(hidden_state, gain_first).astype(jnp.bfloat16)
+
+    normed_all = lax.all_gather(normed, "expert", axis=0, tiled=True)
     gates, target_slot, position, retained = route_rows(
-        normed, w_router, expert_ids, replica_pick, slot_expert, cap_blocks, CAP_UNIT
-    )
-    dest = target_slot // slot_local
-    row_in_hub = (target_slot % slot_local) * slot_rows + exp_at * CAP_MOST + position
-    code = jnp.where(retained, dest * hub_rows + row_in_hub, -1).astype(jnp.int32)
-    kept_gates = jnp.where(retained, gates, jnp.float32(0.0))
-
-    normed_all = lax.all_gather(normed, "expert", axis=0, tiled=True)
-    code_all = lax.all_gather(code, "expert", axis=0, tiled=True)
-    gates_all = lax.all_gather(kept_gates, "expert", axis=0, tiled=True)
-    local = code_all - exp_at * hub_rows
-    valid = (code_all >= 0) & (local >= 0) & (local < hub_rows)
-    local = jnp.where(valid, local, -1)
-    hit = local[:, :, None] == jnp.arange(hub_rows)
-    pick = jnp.any(hit, axis=1).astype(jnp.bfloat16)
-    weight = jnp.sum(jnp.where(hit, gates_all[:, :, None], jnp.float32(0.0)), axis=1)
-    slot_in = lax.dot_general(
-        pick, normed_all, (((0,), (0,)), ((), ())), preferred_element_type=jnp.float32
+        normed_all,
+        w_router,
+        ids_all[:, :, :topk_all],
+        ids_all[:, :, topk_all:],
+        slot_expert,
+        cap_blocks,
+        CAP_UNIT,
+    )
+    here = retained & (target_slot // slot_local == exp_at)
+    local = jnp.where(here, (target_slot % slot_local) * CAP_MOST + position, -1)
+    hit = local[..., None] == jnp.arange(slot_local * CAP_MOST)
+    pick = jnp.any(hit, axis=2).astype(jnp.bfloat16)
+    weight = jnp.sum(jnp.where(hit, gates[..., None], jnp.float32(0.0)), axis=2)
+    slot_in = jnp.einsum(
+        "btr,btd->brd",
+        pick,
+        normed_all.reshape(n_exp, tok_rows, model_width),
+        preferred_element_type=jnp.float32,
     ).astype(jnp.bfloat16)
-    slot_in = slot_in.reshape(slot_local, slot_rows, model_width)
+    slot_in = slot_in.reshape(n_exp, slot_local, CAP_MOST, model_width)
 
     x_parts = []
     for o in range(n_dp):
         x_parts.append(
-            jnp.stack([slot_in[min(first_slot[o] + j, slot_local - 1)] for j in range(slots_per)])
+            jnp.stack(
+                [slot_in[:, min(first_slot[o] + j, slot_local - 1)] for j in range(slots_per)]
+            )
         )
     x_recv = lax.all_to_all(jnp.stack(x_parts), "dp", 0, 0, tiled=True)
 
-    unit_rows = n_dp * slot_rows
+    unit_rows = n_dp * n_exp * CAP_MOST
     y_acc = jnp.zeros((slots_per, unit_rows, model_width), jnp.float32)
     my_first = (dp_at * units_per) // chunks
     for i in range(units_per):
@@ -169,8 +185,8 @@
         y_acc = lax.dynamic_update_index_in_dim(y_acc, prev + out, slot_at, axis=0)
 
     y_send = (
-        y_acc.reshape(slots_per, n_dp, slot_rows, model_width)
-        .transpose(1, 0, 2, 3)
+        y_acc.reshape(slots_per, n_dp, n_exp, CAP_MOST, model_width)
+        .transpose(1, 0, 2, 3, 4)
         .astype(jnp.bfloat16)
     )
     y_recv = lax.all_to_all(y_send, "dp", 0, 0, tiled=True)
@@ -182,15 +198,26 @@
             if s < slot_local and s in mine:
                 part = y_recv[o, j].astype(jnp.float32)
                 slot_out[s] = part if slot_out[s] is None else slot_out[s] + part
-    expert_out = jnp.concatenate(slot_out, axis=0).astype(jnp.bfloat16)
+    expert_out = (
+        jnp.stack(slot_out, axis=1)
+        .reshape(n_exp, slot_local * CAP_MOST, model_width)
+        .astype(jnp.bfloat16)
+    )
 
     weight_hi = weight.astype(jnp.bfloat16)
     weight_lo = (weight - weight_hi.astype(jnp.float32)).astype(jnp.bfloat16)
-    partial = jnp.dot(weight_hi, expert_out, preferred_element_type=jnp.float32) + jnp.dot(
-        weight_lo, expert_out, preferred_element_type=jnp.float32
-    )
-    combined = lax.psum_scatter(partial, "expert", scatter_dimension=0, tiled=True)
-    residual_out = (hidden_state.astype(jnp.float32) + combined).astype(jnp.bfloat16)
+    partial = jnp.einsum(
+        "btr,brd->btd", weight_hi, expert_out, preferred_element_type=jnp.float32
+    ) + jnp.einsum("btr,brd->btd", weight_lo, expert_out, preferred_element_type=jnp.float32)
+    combined = lax.psum_scatter(
+        partial.reshape(n_exp * tok_rows, model_width).astype(jnp.bfloat16),
+        "expert",
+        scatter_dimension=0,
+        tiled=True,
+    )
+    residual_out = (hidden_state.astype(jnp.float32) + combined.astype(jnp.float32)).astype(
+        jnp.bfloat16
+    )
     next_normed = rms_scale(residual_out, gain_next).astype(jnp.bfloat16)
     return (residual_out, next_normed)
 

time: 475 us -> 424 us (0.89)
  other arithmetic: 71.4 us -> 40.2 us
  local copies, waits for them, and re-layouts: 39.7 us -> 64 us
  waiting for transfers between devices: 258 us -> 241 us
  blocking collectives: 29 us -> 14.7 us
  matrix products: 40.7 us -> 31.4 us
    reduce_scatter x1, waiting for transfers between devices: 69.9 us -> 40.5 us  [on_device(): lax.psum_scatter(partial.reshape(n_exp * tok_rows, model_width).astype(jn...]
    all_to_all x1, waiting for transfers between devices: 35.9 us -> 64.7 us  [on_device(): y_recv = lax.all_to_all(y_send, 'dp', 0, 0, tiled=True)]
    reduce_scatter x1, waiting for transfers between devices: 40.8 us -> 14.1 us  [on_device(): lax.psum_scatter(jnp.dot(flat_context, w_proj, preferred_element_type=jnp...]
    reduce_or x1, other arithmetic: 23.7 us -> 1.35 us  [on_device(): pick = jnp.any(hit, axis=2).astype(jnp.bfloat16)]
    all_to_all x2 -> x1, waiting for transfers between devices: 49.2 us -> 70.7 us  [on_device(): lax.all_to_all(jnp.stack([win_send, wout_send.reshape(win_send.shape)], a...]
    reduce_sum x3, other arithmetic: 19 us -> 1.82 us  [the longest x1 1.04 us: on_device(): weight = jnp.sum(jnp.where(hit, gates[..., None], jnp.float32(0.0)), axis=2)]
    another operation x0 -> x8, local copies, waits for them, and re-layouts: none -> 17 us  [the longest x1 8.35 us: on_device(): wout_recv = both_recv[:, :, 1].reshape(wout_send.shape)]
    all_to_all x1, waiting for transfers between devices: 61.6 us -> 46.7 us  [on_device(): x_recv = lax.all_to_all(jnp.stack(x_parts), 'dp', 0, 0, tiled=True)]
  transfers between devices with their start and end apart: 7 -> 6, of which waited for: 6 -> 6; matrix products, arithmetic and copies ran while one was open for 16% -> 16% of each run, Pallas kernels for 0% -> 0%
where the time goes in v2:
time: 424 us; the launch traced here: 422 us
  waiting for transfers between devices  241 us (57%)
  local copies, waits for them, and re-layouts  64 us (15%)
  other arithmetic  40.2 us (9%)
  matrix products  31.4 us (7%)
  starting transfers between devices  17.1 us (4%)
  blocking collectives  14.7 us (3%)
  between operations  14.4 us (3%)
    all_to_all x1, waiting for transfers between devices, on_device(): lax.all_to_all(jnp.stack([win_send, wout_send.reshape(win_send.shape)], a...  70.7 us
    all_to_all x1, waiting for transfers between devices, on_device(): y_recv = lax.all_to_all(y_send, 'dp', 0, 0, tiled=True)  64.7 us
    all_to_all x1, waiting for transfers between devices, on_device(): x_recv = lax.all_to_all(jnp.stack(x_parts), 'dp', 0, 0, tiled=True)  46.7 us
    reduce_scatter x1, waiting for transfers between devices, on_device(): lax.psum_scatter(partial.reshape(n_exp * tok_rows, model_width).astype(jn...  40.5 us
    all_gather x1, blocking collectives, on_device(): lax.all_gather(jnp.concatenate([expert_ids, replica_pick], axis=1), 'expe...  14.7 us
    reduce_scatter x1, waiting for transfers between devices, on_device(): lax.psum_scatter(jnp.dot(flat_context, w_proj, preferred_element_type=jnp...  14.1 us
    another operation x2, other arithmetic, on_device(): jnp.stack([win_send, wout_send.reshape(win_send.shape)], axis=2)  10.1 us
    dot_general x3, matrix products, on_device(): out = jnp.dot(activated, w_down, preferred_element_type=jnp.float32)  8.51 us
  transfers between devices with their start and end apart: 6, of which 6 were waited for; matrix products, arithmetic and copies ran while one was open for 16% of the time, Pallas kernels for 0%

profile of v2, /device:TPU:0, one launch (start us, length us, event | category | flops | bytes accessed | tf_op | source)
XLA Modules:
  0.0 422.4 jit_solution(1580708196196906175)
XLA Ops:
  8.4 3.3 convolution_convert_fusion.1
  31.7 14.1 %reduce-scatter.3.cloned.1.call-done = bf16[128,1536]{1,0:T(8,128)(2,1)} async-done(((bf16[512,1536]{1,0:T(8,128)(2,1)}), bf16[128,1536]{1,0:T(8,128)(2,1)}) %reduce-scatter.3.cloned.1.call-update) | async-done | bytes 393232 | tf_op jit(solution)/shard_map/reduce_scatter | solution.py:124
  49.2 7.6 %maximum_maximum_fusion = bf16[4,3,2,384,512]{4,3,1,2,0:T(8,128)(2,1)} fusion(bf16[1,3,1,384,512]{4,3,1,2,0:T(8,128)(2,1)} %stack.175, bf16[1,3,1,384,512]{4,3,1,2,0:T(8,128)(2,1)S(1)} %stack.173, bf16[1,3,1,384,512]{4,3,1,2,0:T(8,128)(2,1)S(1)} %stack.171, bf16[1,3,1,384,512]{4,3,1,2,0:T(8,128)(2,1)S(1)} %stack.169, ...), kind=kLoop, calls=%fused_computation | loop fusion | flops 18874368 | bytes 18874368 | tf_op jit(solution)/shard_map/stack | solution.py:113
  56.8 6.0 %all-to-all-start.1 = ((bf16[4,3,2,384,512]{4,3,1,2,0:T(8,128)(2,1)}), bf16[4,3,2,384,512]{4,3,1,2,0:T(8,128)(2,1)}, u32[]{:S(2)}, u32[]{:S(2)}) async-start(bf16[4,3,2,384,512]{4,3,1,2,0:T(8,128)(2,1)} %maximum_maximum_fusion), calls=%async_computation.2 | async-start | bytes 18874368 | tf_op jit(solution)/shard_map/all_to_all | solution.py:112
  62.8 14.7 %all_gather.6 = s32[1024,16]{0,1:T(8,128)S(1)} all-gather(s32[128,16]{0,1:T(8,128)S(1)} %pad_add_fusion), channel_id=1, replica_groups=mesh['dp'=4,'expert'=8] {'expert'}, dimensions={0}, use_global_device_ids=true | all-gather | bytes 73728 | tf_op jit(solution)/shard_map/all_gather | solution.py:119
  84.3 3.8 all-gather.2.cloned.1.call-done
  88.1 3.3 convolution_convert_fusion
  92.4 3.4 pad_maximum_fusion
  95.8 70.7 %all-to-all-done.1 = bf16[4,3,2,384,512]{4,3,1,2,0:T(8,128)(2,1)} async-done(((bf16[4,3,2,384,512]{4,3,1,2,0:T(8,128)(2,1)}), bf16[4,3,2,384,512]{4,3,1,2,0:T(8,128)(2,1)}, u32[]{:S(2)}, u32[]{:S(2)}) %all-to-all-start.1) | async-done | bytes 9437216 | tf_op jit(solution)/shard_map/all_to_all | solution.py:112
  166.5 5.4 %all-to-all-start = ((bf16[4,2,8,32,1536]{4,3,2,1,0:T(8,128)(2,1)}), bf16[4,2,8,32,1536]{4,3,2,1,0:T(8,128)(2,1)}, u32[]{:S(2)}, u32[]{:S(2)}) async-start(bf16[4,2,8,32,1536]{4,3,2,1,0:T(8,128)(2,1)} %pad_maximum_fusion), calls=%async_computation.1 | async-start | bytes 12582912 | tf_op jit(solution)/shard_map/all_to_all | solution.py:165
  172.0 8.3 %slice_bitcast_fusion = (bf16[3,4,384,512]{3,2,0,1:T(8,128)(2,1)}, bf16[4,3,1,384,512]{4,3,1,2,0:T(8,128)(2,1)}) fusion(bf16[4,3,2,384,512]{4,3,1,2,0:T(8,128)(2,1)} %all-to-all-done.1), kind=kLoop, calls=%fused_computation.11 | loop fusion | bytes 18874368 | tf_op jit(solution)/shard_map/transpose | solution.py:117
  180.3 8.3 %reshape_squeeze.3 = bf16[4,3,128,1536]{3,2,1,0:T(8,128)(2,1)} reshape(bf16[4,3,1,384,512]{4,3,1,2,0:T(8,128)(2,1)} %get-tuple-element.7) | data formatting | bytes 9437184 | tf_op jit(solution)/shard_map/reshape;squeeze | solution.py:116
  194.4 46.7 %all-to-all-done = bf16[4,2,8,32,1536]{4,3,2,1,0:T(8,128)(2,1)} async-done(((bf16[4,2,8,32,1536]{4,3,2,1,0:T(8,128)(2,1)}), bf16[4,2,8,32,1536]{4,3,2,1,0:T(8,128)(2,1)}, u32[]{:S(2)}, u32[]{:S(2)}) %all-to-all-start) | async-done | bytes 6291488 | tf_op jit(solution)/shard_map/all_to_all | solution.py:165
  241.1 4.9 %constant_dynamic-slice_fusion = (bf16[4,1,8,32,1536]{4,3,2,1,0:T(8,128)(2,1)S(1)}, bf16[4,1,8,32,1536]{4,3,2,1,0:T(8,128)(2,1)S(1)}, bf16[4,1,8,32,1536]{4,3,2,1,0:T(8,128)(2,1)S(1)}) fusion(bf16[4,2,8,32,1536]{4,3,2,1,0:T(8,128)(2,1)} %all-to-all-done, s32[]{:T(128)S(6)} %select_n.128, s32[]{:T(128)S(6)} %select_n.124), kind=kLoop, calls=%fused_computation.152 | loop fusion | bytes 18874376 | tf_op jit(solution)/shard_map/jit(dynamic_index_in_dim)/dynamic_slice | solution.py:174
  246.1 4.6 %fusion.58 = f32[1024,512]{1,0:T(8,128)} fusion(bf16[1024,1536]{1,0:T(8,128)(2,1)S(1)} %bitcast.222, bf16[1536,512]{1,0:T(8,128)(2,1)} %bitcast.227), kind=kOutput, calls=%fused_computation.169 | convolution fusion | flops 1610612736 | bytes 6815744 | tf_op jit(solution)/shard_map/dot_general | solution.py:179
  253.5 5.8 %dynamic_update_slice.10 = f32[2,1024,1536]{2,1,0:T(8,128)} pad(f32[1,1024,1536]{2,1,0:T(8,128)S(1)} %convolution_bitcast_fusion, f32[]{:T(128)} %constant.123.clone.1), padding=0_1x0_0x0_0 | pad | bytes 18874372 | tf_op jit(solution)/shard_map/jit(dynamic_update_index_in_dim)/dynamic_update_slice | solution.py:185
  259.2 3.8 bitcast_dynamic-update-slice_fusion.1
  263.1 3.3 constant_dynamic-slice_fusion.1
  268.2 3.7 bitcast_dynamic-update-slice_fusion
  271.9 8.0 %convert_element_type.190 = bf16[2,1024,1536]{2,1,0:T(8,128)(2,1)} convert(f32[2,1024,1536]{2,1,0:T(8,128)} %bitcast_dynamic-update-slice_fusion) | non-fusion elementwise | flops 3145728 | bytes 18874368 | tf_op jit(solution)/shard_map/convert_element_type | solution.py:190
  279.9 6.2 %copy.107 = bf16[2,4,8,32,1536]{4,3,2,0,1:T(8,128)(2,1)} copy(bf16[2,4,8,32,1536]{4,3,2,1,0:T(8,128)(2,1)} %bitcast.214) | data formatting | bytes 12582912 | tf_op jit(solution)/shard_map/convert_element_type | solution.py:190
  286.1 5.4 %all-to-all-start.2 = ((bf16[4,2,8,32,1536]{4,3,2,1,0:T(8,128)(2,1)}), bf16[4,2,8,32,1536]{4,3,2,1,0:T(8,128)(2,1)}, u32[]{:S(2)}, u32[]{:S(2)}) async-start(bf16[4,2,8,32,1536]{4,3,2,1,0:T(8,128)(2,1)} %bitcast.213), calls=%async_computation.3 | async-start | bytes 12582912 | tf_op jit(solution)/shard_map/all_to_all | solution.py:192
  296.1 64.7 %all-to-all-done.2 = bf16[4,2,8,32,1536]{4,3,2,1,0:T(8,128)(2,1)} async-done(((bf16[4,2,8,32,1536]{4,3,2,1,0:T(8,128)(2,1)}), bf16[4,2,8,32,1536]{4,3,2,1,0:T(8,128)(2,1)}, u32[]{:S(2)}, u32[]{:S(2)}) %all-to-all-start.2) | async-done | bytes 6291488 | tf_op jit(solution)/shard_map/all_to_all | solution.py:192
  373.1 40.5 %reduce-scatter.5.cloned.1.call-done = bf16[128,1536]{1,0:T(8,128)(2,1)} async-done(((bf16[1024,1536]{1,0:T(8,128)(2,1)}), bf16[128,1536]{1,0:T(8,128)(2,1)}) %reduce-scatter.5.cloned.1.call-update) | async-done | bytes 393232 | tf_op jit(solution)/shard_map/reduce_scatter | solution.py:212
  (117 shorter events, 61.5 us)
Async XLA Ops:
  7.2 1.3 copy-start
  7.2 38.6 %reduce-scatter.3.cloned.1.call-start = ((), (), s32[]{:S(2)}) async-start(), calls=%async_computation.5 | async-start | bytes 1966080 | tf_op jit(solution)/shard_map/reduce_scatter | solution.py:124
  8.4 3.4 copy-start.2
  11.8 76.3 %all-gather.2.cloned.1.call-start = ((), (), s32[]{:S(2)}) async-start(), calls=%async_computation.6 | async-start | bytes 3538944 | tf_op jit(solution)/shard_map/all_gather | solution.py:135
  29.2 18.0 %copy-start.10 = (f32[1536]{0:T(1024)S(1)}, f32[1536]{0:T(1024)}, u32[]{:S(2)}) copy-start(f32[1536]{0:T(1024)} %param.15) | copy-start | bytes 18436
  56.8 6.0 %copy-start.13 = (s32[128,8]{0,1:T(8,128)S(1)}, s32[128,8]{0,1:T(8,128)}, u32[]{:S(2)}) copy-start(s32[128,8]{0,1:T(8,128)} %param.19) | copy-start | bytes 12292
  56.8 6.0 %copy-start.14 = (s32[128,8]{0,1:T(8,128)S(1)}, s32[128,8]{0,1:T(8,128)}, u32[]{:S(2)}) copy-start(s32[128,8]{0,1:T(8,128)} %param.18) | copy-start | bytes 12292
  56.8 21.0 %copy-start.12 = (s32[48]{0:T(128)S(1)}, s32[48]{0:T(128)}, u32[]{:S(2)}) copy-start(s32[48]{0:T(128)} %param.20) | copy-start | bytes 580
  56.8 109.6 %all-to-all-start.1 = ((bf16[4,3,2,384,512]{4,3,1,2,0:T(8,128)(2,1)}), bf16[4,3,2,384,512]{4,3,1,2,0:T(8,128)(2,1)}, u32[]{:S(2)}, u32[]{:S(2)}) async-start(bf16[4,3,2,384,512]{4,3,1,2,0:T(8,128)(2,1)} %maximum_maximum_fusion), calls=%async_computation.2 | async-start | bytes 18874368 | tf_op jit(solution)/shard_map/all_to_all | solution.py:112
  79.7 2.7 copy-start.15
  166.5 74.6 %all-to-all-start = ((bf16[4,2,8,32,1536]{4,3,2,1,0:T(8,128)(2,1)}), bf16[4,2,8,32,1536]{4,3,2,1,0:T(8,128)(2,1)}, u32[]{:S(2)}, u32[]{:S(2)}) async-start(bf16[4,2,8,32,1536]{4,3,2,1,0:T(8,128)(2,1)} %pad_maximum_fusion), calls=%async_computation.1 | async-start | bytes 12582912 | tf_op jit(solution)/shard_map/all_to_all | solution.py:165
  180.3 11.4 %slice-start = ((s8[4718592]{0:T(1024)(128)(4,1)}), s8[524288]{0:T(1024)(128)(4,1)S(1)}, s32[]{:S(2)}) async-start(s8[4718592]{0:T(1024)(128)(4,1)} %bitcast.217), calls=%async_computation.8 | async-start | bytes 1048576
  188.6 3.6 slice-start.1
  246.0 4.6 %copy-start.6 = (bf16[1,4,384,512]{3,2,0,1:T(8,128)(2,1)S(1)}, bf16[1,4,384,512]{3,2,0,1:T(8,128)(2,1)}, u32[]{:S(2)}) copy-start(bf16[1,4,384,512]{3,2,0,1:T(8,128)(2,1)} %get-tuple-element.13) | copy-start | bytes 4718596
  253.5 5.8 %copy-start.8 = (f32[1024,512]{1,0:T(8,128)S(1)}, f32[1024,512]{1,0:T(8,128)}, u32[]{:S(2)}) copy-start(f32[1024,512]{1,0:T(8,128)} %fusion.58) | copy-start | bytes 6291460
  263.1 3.4 copy-start.5
  286.1 5.7 %copy-start.9 = (bf16[1536,40]{0,1:T(8,128)(2,1)S(1)}, bf16[1536,40]{0,1:T(8,128)(2,1)}, u32[]{:S(2)}) copy-start(bf16[1536,40]{0,1:T(8,128)(2,1)} %param.17) | copy-start | bytes 368644
  286.1 74.7 %all-to-all-start.2 = ((bf16[4,2,8,32,1536]{4,3,2,1,0:T(8,128)(2,1)}), bf16[4,2,8,32,1536]{4,3,2,1,0:T(8,128)(2,1)}, u32[]{:S(2)}, u32[]{:S(2)}) async-start(bf16[4,2,8,32,1536]{4,3,2,1,0:T(8,128)(2,1)} %bitcast.213), calls=%async_computation.3 | async-start | bytes 12582912 | tf_op jit(solution)/shard_map/all_to_all | solution.py:192
  291.5 122.1 %reduce-scatter.5.cloned.1.call-start = ((), (), s32[]{:S(2)}) async-start(), calls=%async_computation.7 | async-start | bytes 3538944 | tf_op jit(solution)/shard_map/reduce_scatter | solution.py:212
  373.0 40.6 %copy-start.3 = (bf16[128,1536]{1,0:T(8,128)(2,1)S(1)}, bf16[128,1536]{1,0:T(8,128)(2,1)}, u32[]{:S(2)}) copy-start(bf16[128,1536]{1,0:T(8,128)(2,1)} %param.14) | copy-start | bytes 1179652
  373.1 40.6 %copy-start.4 = (bf16[128,1536]{1,0:T(8,128)(2,1)S(1)}, bf16[128,1536]{1,0:T(8,128)(2,1)}, u32[]{:S(2)}) copy-start(bf16[128,1536]{1,0:T(8,128)(2,1)} %reduce-scatter.3.cloned.1.call-done) | copy-start | bytes 1179652
  373.1 42.8 %copy-start.1 = (bf16[384,1536]{1,0:T(8,128)(2,1)S(1)}, bf16[384,1536]{1,0:T(8,128)(2,1)}, u32[]{:S(2)}) copy-start(bf16[384,1536]{1,0:T(8,128)(2,1)} %param.13) | copy-start | bytes 3538948
  373.1 41.9 %copy-start.11 = (f32[1536]{0:T(1024)S(1)}, f32[1536]{0:T(1024)}, u32[]{:S(2)}) copy-start(f32[1536]{0:T(1024)} %param.16) | copy-start | bytes 18436
  414.9 0.9 copy-start.7
Sparse Core Ops, SparseCore 0:
  11.9 33.8 reduce-scatter.2
  49.3 38.7 all-gather.1
  373.2 40.3 reduce-scatter.4

commit v3 on v2

--- a/solution.py
+++ b/solution.py
@@ -54,14 +54,17 @@
 
 
 def unit_plan(slot_local, n_dp, hidden_units):
-    chunks = n_dp // math.gcd(slot_local, n_dp)
-    units_per = slot_local * chunks // n_dp
+    full = slot_local // n_dp
+    rest = slot_local - full * n_dp
+    chunks = n_dp // math.gcd(rest, n_dp) if rest else 1
+    halves = rest * chunks // n_dp
     chunk_width = hidden_units // chunks
-    owned = [[((o * units_per + i) // chunks, (o * units_per + i) % chunks) for i in range(units_per)]
-             for o in range(n_dp)]
-    first_slot = [owned[o][0][0] for o in range(n_dp)]
-    slots_per = max(owned[o][-1][0] - first_slot[o] + 1 for o in range(n_dp))
-    return chunks, units_per, chunk_width, owned, first_slot, slots_per
+    owned_full = [[o * full + j for j in range(full)] for o in range(n_dp)]
+    owned_part = [
+        [(full * n_dp + (o * halves + i) // chunks, (o * halves + i) % chunks) for i in range(halves)]
+        for o in range(n_dp)
+    ]
+    return full, halves, chunks, chunk_width, owned_full, owned_part
 
 
 def on_device(
@@ -87,34 +90,49 @@
     n_exp = lax.axis_size("expert")
     dp_at = lax.axis_index("dp")
     exp_at = lax.axis_index("expert")
-    chunks, units_per, chunk_width, owned, first_slot, slots_per = unit_plan(
+    full, halves, chunks, chunk_width, owned_full, owned_part = unit_plan(
         slot_local, n_dp, hidden_units
     )
     sources_per_chunk = chunk_width // ff_local
-
-    win_parts, wout_parts = [], []
+    lane_width = 2 * chunk_width if (ff_local * model_width) % (2 * chunk_width) == 0 else 128
+
+    def as_rows(piece):
+        return piece.reshape(-1, lane_width)
+
+    weight_parts = []
     for o in range(n_dp):
-        win_units, wout_units = [], []
-        for s, c in owned[o]:
+        pieces = []
+        for s in owned_full[o]:
+            pieces += [as_rows(w_in[s]), as_rows(w_out[s])]
+        for s, c in owned_part[o]:
             lo = c * chunk_width
-            win_units.append(
-                jnp.concatenate(
-                    [w_in[s, :, lo:lo + chunk_width],
-                     w_in[s, :, hidden_units + lo:hidden_units + lo + chunk_width]],
-                    axis=-1,
-                )
-            )
-            wout_units.append(w_out[s])
-        win_parts.append(jnp.stack(win_units))
-        wout_parts.append(jnp.stack(wout_units))
-    win_send = jnp.stack(win_parts)
-    wout_send = jnp.stack(wout_parts)
-    both_recv = lax.all_to_all(
-        jnp.stack([win_send, wout_send.reshape(win_send.shape)], axis=2), "dp", 0, 0, tiled=True
-    )
-    win_recv = both_recv[:, :, 0]
-    wout_recv = both_recv[:, :, 1].reshape(wout_send.shape)
-    unit_in = win_recv.transpose(1, 0, 2, 3).reshape(units_per, n_dp * d_local, 2 * chunk_width)
+            pieces += [
+                as_rows(w_in[s, :, lo:lo + chunk_width]),
+                as_rows(w_in[s, :, hidden_units + lo:hidden_units + lo + chunk_width]),
+                as_rows(w_out[s]),
+            ]
+        weight_parts.append(jnp.concatenate(pieces, axis=0))
+    weight_recv = lax.all_to_all(jnp.stack(weight_parts), "dp", 0, 0, tiled=True)
+    offset = 0
+
+    def take(shape):
+        nonlocal offset
+        count = math.prod(shape) // lane_width
+        piece = weight_recv[:, offset:offset + count].reshape((n_dp,) + shape)
+        offset += count
+        return piece
+
+    full_in, full_out, part_in, part_out = [], [], [], []
+    for _ in range(full):
+        full_in.append(take((d_local, 2 * hidden_units)).reshape(n_dp * d_local, 2 * hidden_units))
+        full_out.append(take((ff_local, model_width)).reshape(n_dp * ff_local, model_width))
+    for _ in range(halves):
+        gate_in = take((d_local, chunk_width))
+        up_in = take((d_local, chunk_width))
+        part_in.append(
+            jnp.concatenate([gate_in, up_in], axis=-1).reshape(n_dp * d_local, 2 * chunk_width)
+        )
+        part_out.append(take((ff_local, model_width)))
 
     ids_all = lax.all_gather(
         jnp.concatenate([expert_ids, replica_pick], axis=1), "expert", axis=0, tiled=True
@@ -158,46 +176,42 @@
     x_parts = []
     for o in range(n_dp):
         x_parts.append(
-            jnp.stack(
-                [slot_in[:, min(first_slot[o] + j, slot_local - 1)] for j in range(slots_per)]
-            )
+            jnp.stack([slot_in[:, s] for s in owned_full[o]] + [slot_in[:, s] for s, _ in owned_part[o]])
         )
     x_recv = lax.all_to_all(jnp.stack(x_parts), "dp", 0, 0, tiled=True)
 
     unit_rows = n_dp * n_exp * CAP_MOST
-    y_acc = jnp.zeros((slots_per, unit_rows, model_width), jnp.float32)
-    my_first = (dp_at * units_per) // chunks
-    for i in range(units_per):
-        unit = dp_at * units_per + i
-        slot_at = unit // chunks - my_first
-        chunk_at = unit % chunks
-        rows = lax.dynamic_index_in_dim(x_recv, slot_at, axis=1, keepdims=False)
-        rows = rows.reshape(unit_rows, model_width)
+
+    def expert_rows(rows, w_up, w_down, width):
+        gate_up = jnp.dot(rows, w_up, preferred_element_type=jnp.float32)
+        activated = (jax.nn.silu(gate_up[:, :width]) * gate_up[:, width:]).astype(jnp.bfloat16)
+        return jnp.dot(activated, w_down, preferred_element_type=jnp.float32).astype(jnp.bfloat16)
+
+    outs = []
+    for j in range(full):
+        rows = x_recv[:, j].reshape(unit_rows, model_width)
+        outs.append(expert_rows(rows, full_in[j], full_out[j], hidden_units))
+    for i in range(halves):
+        rows = x_recv[:, full + i].reshape(unit_rows, model_width)
+        chunk_at = (dp_at * halves + i) % chunks
         w_down = lax.dynamic_slice_in_dim(
-            wout_recv[:, i], chunk_at * sources_per_chunk, sources_per_chunk, axis=0
+            part_out[i], chunk_at * sources_per_chunk, sources_per_chunk, axis=0
         ).reshape(chunk_width, model_width)
-        gate_up = jnp.dot(rows, unit_in[i], preferred_element_type=jnp.float32)
-        activated = (
-            jax.nn.silu(gate_up[:, :chunk_width]) * gate_up[:, chunk_width:]
-        ).astype(jnp.bfloat16)
-        out = jnp.dot(activated, w_down, preferred_element_type=jnp.float32)
-        prev = lax.dynamic_index_in_dim(y_acc, slot_at, axis=0, keepdims=False)
-        y_acc = lax.dynamic_update_index_in_dim(y_acc, prev + out, slot_at, axis=0)
-
+        outs.append(expert_rows(rows, part_in[i], w_down, chunk_width))
     y_send = (
-        y_acc.reshape(slots_per, n_dp, n_exp, CAP_MOST, model_width)
+        jnp.stack(outs)
+        .reshape(full + halves, n_dp, n_exp, CAP_MOST, model_width)
         .transpose(1, 0, 2, 3, 4)
-        .astype(jnp.bfloat16)
     )
     y_recv = lax.all_to_all(y_send, "dp", 0, 0, tiled=True)
     slot_out = [None] * slot_local
     for o in range(n_dp):
-        mine = {s for s, _ in owned[o]}
-        for j in range(slots_per):
-            s = first_slot[o] + j
-            if s < slot_local and s in mine:
-                part = y_recv[o, j].astype(jnp.float32)
-                slot_out[s] = part if slot_out[s] is None else slot_out[s] + part
+        for j, s in enumerate(owned_full[o]):
+            slot_out[s] = y_recv[o, j]
+        for i, (s, _) in enumerate(owned_part[o]):
+            part = y_recv[o, full + i].astype(jnp.float32)
+            slot_out[s] = part if slot_out[s] is None else slot_out[s] + part
+    slot_out = [part.astype(jnp.bfloat16) for part in slot_out]
     expert_out = (
         jnp.stack(slot_out, axis=1)
         .reshape(n_exp, slot_local * CAP_MOST, model_width)
@@ -210,7 +224,7 @@
         "btr,brd->btd", weight_hi, expert_out, preferred_element_type=jnp.float32
     ) + jnp.einsum("btr,brd->btd", weight_lo, expert_out, preferred_element_type=jnp.float32)
     combined = lax.psum_scatter(
-        partial.reshape(n_exp * tok_rows, model_width).astype(jnp.bfloat16),
+        partial.reshape(n_exp * tok_rows, model_width),
         "expert",
         scatter_dimension=0,
         tiled=True,

time: 424 us -> 411 us (0.969)
  other arithmetic: 40.2 us -> 27 us
  local copies, waits for them, and re-layouts: 64 us -> 72 us
  matrix products: 31.4 us -> 23.6 us
    reduce_scatter x1, waiting for transfers between devices: 40.5 us -> 69.9 us  [on_device(): lax.psum_scatter(partial.reshape(n_exp * tok_rows, model_width), 'expert'...]
    another operation x6 -> x21, local copies, waits for them, and re-layouts: 15.3 us -> 30.4 us  [the longest x18 20.5 us: as_rows(): return piece.reshape(-1, lane_width)]
    all_to_all x1, waiting for transfers between devices: 70.7 us -> 57.2 us  [on_device(): lax.all_to_all(jnp.stack(weight_parts), 'dp', 0, 0, tiled=True)]
    reduce_scatter x1, waiting for transfers between devices: 14.1 us -> 2.73 us  [on_device(): lax.psum_scatter(jnp.dot(flat_context, w_proj, preferred_element_type=jnp...]
    slice x4 -> x7, local copies, waits for them, and re-layouts: 7.47 us -> 17.8 us  [the longest x3 8.72 us: take(): piece = weight_recv[:, offset:offset + count].reshape((n_dp,) + shape)]
    unnamed x40 -> x83, local copies, waits for them, and re-layouts: 5.44 us -> 15.6 us
    dot_general x6 -> x4, matrix products: 16.7 us -> 8.03 us  [the longest x2 5.19 us: expert_rows(): gate_up = jnp.dot(rows, w_up, preferred_element_type=jnp.float32)]
    transpose x1 -> x0, local copies, waits for them, and re-layouts: 8.26 us -> none  [on_device(): win_recv.transpose(1, 0, 2, 3)]
  transfers between devices with their start and end apart: 6 -> 6, of which waited for: 6 -> 6; matrix products, arithmetic and copies ran while one was open for 16% -> 21% of each run, Pallas kernels for 0% -> 0%
where the time goes in v3:
time: 411 us; the launch traced here: 409 us
  waiting for transfers between devices  241 us (59%)
  local copies, waits for them, and re-layouts  72 us (18%)
  other arithmetic  27 us (7%)
  matrix products  23.6 us (6%)
  starting transfers between devices  17 us (4%)
  blocking collectives  14.7 us (4%)
  between operations  14.4 us (4%)
    reduce_scatter x1, waiting for transfers between devices, on_device(): lax.psum_scatter(partial.reshape(n_exp * tok_rows, model_width), 'expert'...  69.9 us
    all_to_all x1, waiting for transfers between devices, on_device(): y_recv = lax.all_to_all(y_send, 'dp', 0, 0, tiled=True)  64.7 us
    all_to_all x1, waiting for transfers between devices, on_device(): lax.all_to_all(jnp.stack(weight_parts), 'dp', 0, 0, tiled=True)  57.2 us
    all_to_all x1, waiting for transfers between devices, on_device(): x_recv = lax.all_to_all(jnp.stack(x_parts), 'dp', 0, 0, tiled=True)  45.9 us
    another operation x18, local copies, waits for them, and re-layouts, as_rows(): return piece.reshape(-1, lane_width)  20.5 us
    unnamed x83, local copies, waits for them, and re-layouts  15.6 us
    all_gather x1, blocking collectives, on_device(): lax.all_gather(jnp.concatenate([expert_ids, replica_pick], axis=1), 'expe...  14.7 us
    slice x3, local copies, waits for them, and re-layouts, take(): piece = weight_recv[:, offset:offset + count].reshape((n_dp,) + shape)  8.72 us
  transfers between devices with their start and end apart: 6, of which 6 were waited for; matrix products, arithmetic and copies ran while one was open for 21% of the time, Pallas kernels for 0%

profile of v3, /device:TPU:0, one launch (start us, length us, event | category | flops | bytes accessed | tf_op | source)
XLA Modules:
  0.0 409.4 jit_solution(10336887826829885044)
XLA Ops:
  8.4 3.1 convolution_convert_fusion.3
  11.7 2.3 fusion.60
  31.1 2.2 fusion.61
  42.9 2.7 reduce-scatter.3.cloned.1.call-done
  54.2 6.1 %pad_maximum_fusion = bf16[4,1920,512]{2,1,0:T(8,128)(2,1)} fusion(bf16[1,1920,512]{2,1,0:T(8,128)(2,1)} %bitcast.19, bf16[1,1920,512]{2,1,0:T(8,128)(2,1)} %bitcast.18, bf16[1,1920,512]{2,1,0:T(8,128)(2,1)S(1)} %bitcast.110, bf16[1,1920,512]{2,1,0:T(8,128)(2,1)S(1)} %bitcast.111), kind=kLoop, calls=%fused_computation | loop fusion | flops 11796480 | bytes 15728640 | tf_op jit(solution)/shard_map/stack | solution.py:115
  60.3 5.7 %all-to-all-start.1 = ((bf16[4,1920,512]{2,1,0:T(8,128)(2,1)}), bf16[4,1920,512]{2,1,0:T(8,128)(2,1)}, u32[]{:S(2)}, u32[]{:S(2)}) async-start(bf16[4,1920,512]{2,1,0:T(8,128)(2,1)} %pad_maximum_fusion), calls=%async_computation.2 | async-start | bytes 15728640 | tf_op jit(solution)/shard_map/all_to_all | solution.py:115
  66.0 14.7 %all_gather.6 = s32[1024,16]{0,1:T(8,128)S(1)} all-gather(s32[128,16]{0,1:T(8,128)S(1)} %pad_add_fusion), channel_id=1, replica_groups=mesh['dp'=4,'expert'=8] {'expert'}, dimensions={0}, use_global_device_ids=true | all-gather | bytes 73728 | tf_op jit(solution)/shard_map/all_gather | solution.py:137
  87.7 3.3 convolution_convert_fusion
  92.0 3.5 pad_maximum_fusion.1
  95.5 57.2 %all-to-all-done.1 = bf16[4,1920,512]{2,1,0:T(8,128)(2,1)} async-done(((bf16[4,1920,512]{2,1,0:T(8,128)(2,1)}), bf16[4,1920,512]{2,1,0:T(8,128)(2,1)}, u32[]{:S(2)}, u32[]{:S(2)}) %all-to-all-start.1) | async-done | bytes 7864352 | tf_op jit(solution)/shard_map/all_to_all | solution.py:115
  152.8 5.5 %all-to-all-start = ((bf16[4,2,8,32,1536]{4,3,2,1,0:T(8,128)(2,1)}), bf16[4,2,8,32,1536]{4,3,2,1,0:T(8,128)(2,1)}, u32[]{:S(2)}, u32[]{:S(2)}) async-start(bf16[4,2,8,32,1536]{4,3,2,1,0:T(8,128)(2,1)} %pad_maximum_fusion.1), calls=%async_computation.1 | async-start | bytes 12582912 | tf_op jit(solution)/shard_map/all_to_all | solution.py:181
  162.2 3.4 fusion.57
  165.6 3.7 reshape_reshape.7
  169.3 3.8 slice.193
  173.1 5.7 %reshape_reshape.6 = bf16[1536,1024]{1,0:T(8,128)(2,1)} reshape(bf16[4,768,512]{2,1,0:T(8,128)(2,1)} %slice.193) | data formatting | bytes 6291456 | tf_op jit(solution)/shard_map/reshape;reshape | solution.py:127
  181.6 45.9 %all-to-all-done = bf16[4,2,8,32,1536]{4,3,2,1,0:T(8,128)(2,1)} async-done(((bf16[4,2,8,32,1536]{4,3,2,1,0:T(8,128)(2,1)}), bf16[4,2,8,32,1536]{4,3,2,1,0:T(8,128)(2,1)}, u32[]{:S(2)}, u32[]{:S(2)}) %all-to-all-start) | async-done | bytes 6291488 | tf_op jit(solution)/shard_map/all_to_all | solution.py:181
  227.5 3.4 fusion.59
  231.2 3.4 fusion.64
  239.3 3.2 maximum_bitcast_fusion
  242.5 5.4 %all-to-all-start.2 = ((bf16[4,2,8,32,1536]{4,3,2,1,0:T(8,128)(2,1)}), bf16[4,2,8,32,1536]{4,3,2,1,0:T(8,128)(2,1)}, u32[]{:S(2)}, u32[]{:S(2)}) async-start(bf16[4,2,8,32,1536]{4,3,2,1,0:T(8,128)(2,1)} %maximum_bitcast_fusion), calls=%async_computation.3 | async-start | bytes 12582912 | tf_op jit(solution)/shard_map/all_to_all | solution.py:206
  248.2 2.9 convolution_bitcast_fusion
  252.6 64.7 %all-to-all-done.2 = bf16[4,2,8,32,1536]{4,3,2,1,0:T(8,128)(2,1)} async-done(((bf16[4,2,8,32,1536]{4,3,2,1,0:T(8,128)(2,1)}), bf16[4,2,8,32,1536]{4,3,2,1,0:T(8,128)(2,1)}, u32[]{:S(2)}, u32[]{:S(2)}) %all-to-all-start.2) | async-done | bytes 6291488 | tf_op jit(solution)/shard_map/all_to_all | solution.py:206
  326.8 3.7 convolution_add_fusion
  330.6 69.9 %reduce-scatter.5.cloned.1.call-done = f32[128,1536]{1,0:T(8,128)} async-done(((f32[1024,1536]{1,0:T(8,128)}), f32[128,1536]{1,0:T(8,128)}) %reduce-scatter.5.cloned.1.call-update) | async-done | bytes 786448 | tf_op jit(solution)/shard_map/reduce_scatter | solution.py:226
  (157 shorter events, 69.4 us)
Async XLA Ops:
  7.2 38.5 %reduce-scatter.3.cloned.1.call-start = ((), (), s32[]{:S(2)}) async-start(), calls=%async_computation.5 | async-start | bytes 1966080 | tf_op jit(solution)/shard_map/reduce_scatter | solution.py:142
  11.6 76.1 %all-gather.2.cloned.1.call-start = ((), (), s32[]{:S(2)}) async-start(), calls=%async_computation.6 | async-start | bytes 3538944 | tf_op jit(solution)/shard_map/all_gather | solution.py:153
  14.0 8.0 %copy-start.8 = (bf16[6,128,1536]{2,1,0:T(8,128)(2,1)S(1)}, bf16[6,128,1536]{2,1,0:T(8,128)(2,1)}, u32[]{:S(2)}) copy-start(bf16[6,128,1536]{2,1,0:T(8,128)(2,1)} %param.23) | copy-start | bytes 7077892
  23.1 5.1 %copy-start.13 = (bf16[1,128,1536]{2,1,0:T(8,128)(2,1)S(1)}, bf16[1,128,1536]{2,1,0:T(8,128)(2,1)}, u32[]{:S(2)}) copy-start(bf16[1,128,1536]{2,1,0:T(8,128)(2,1)} %get-tuple-element.33) | copy-start | bytes 1179652
  39.4 2.7 copy-start.11
  40.3 5.3 %copy-start.2 = (bf16[128,1536]{1,0:T(8,128)(2,1)S(1)}, bf16[128,1536]{1,0:T(8,128)(2,1)}, u32[]{:S(2)}) copy-start(bf16[128,1536]{1,0:T(8,128)(2,1)} %param.14) | copy-start | bytes 1179652
  40.4 6.5 %copy-start.26 = (f32[1536]{0:T(1024)S(1)}, f32[1536]{0:T(1024)}, u32[]{:S(2)}) copy-start(f32[1536]{0:T(1024)} %param.15) | copy-start | bytes 18436
  42.1 10.1 %copy-start.5 = (bf16[768,512]{1,0:T(8,128)(2,1)S(1)}, bf16[768,512]{1,0:T(8,128)(2,1)}, u32[]{:S(2)}) copy-start(bf16[768,512]{1,0:T(8,128)(2,1)} %reshape_squeeze.63) | copy-start | bytes 2359300
  48.8 3.5 copy-start.19
  48.8 3.5 copy-start.23
  48.8 3.5 copy-start.24
  60.3 5.7 %copy-start.29 = (s32[128,8]{0,1:T(8,128)S(1)}, s32[128,8]{0,1:T(8,128)}, u32[]{:S(2)}) copy-start(s32[128,8]{0,1:T(8,128)} %param.19) | copy-start | bytes 12292
  60.3 5.7 %copy-start.30 = (s32[128,8]{0,1:T(8,128)S(1)}, s32[128,8]{0,1:T(8,128)}, u32[]{:S(2)}) copy-start(s32[128,8]{0,1:T(8,128)} %param.18) | copy-start | bytes 12292
  60.3 20.7 %copy-start.28 = (s32[48]{0:T(128)S(1)}, s32[48]{0:T(128)}, u32[]{:S(2)}) copy-start(s32[48]{0:T(128)} %param.20) | copy-start | bytes 580
  60.3 92.5 %all-to-all-start.1 = ((bf16[4,1920,512]{2,1,0:T(8,128)(2,1)}), bf16[4,1920,512]{2,1,0:T(8,128)(2,1)}, u32[]{:S(2)}, u32[]{:S(2)}) async-start(bf16[4,1920,512]{2,1,0:T(8,128)(2,1)} %pad_maximum_fusion), calls=%async_computation.2 | async-start | bytes 15728640 | tf_op jit(solution)/shard_map/all_to_all | solution.py:115
  152.8 74.7 %all-to-all-start = ((bf16[4,2,8,32,1536]{4,3,2,1,0:T(8,128)(2,1)}), bf16[4,2,8,32,1536]{4,3,2,1,0:T(8,128)(2,1)}, u32[]{:S(2)}, u32[]{:S(2)}) async-start(bf16[4,2,8,32,1536]{4,3,2,1,0:T(8,128)(2,1)} %pad_maximum_fusion.1), calls=%async_computation.1 | async-start | bytes 12582912 | tf_op jit(solution)/shard_map/all_to_all | solution.py:181
  227.5 3.7 copy-start.4
  231.2 3.4 copy-start.9
  242.5 5.7 %copy-start.25 = (bf16[1536,40]{0,1:T(8,128)(2,1)S(1)}, bf16[1536,40]{0,1:T(8,128)(2,1)}, u32[]{:S(2)}) copy-start(bf16[1536,40]{0,1:T(8,128)(2,1)} %param.17) | copy-start | bytes 368644
  242.5 74.8 %all-to-all-start.2 = ((bf16[4,2,8,32,1536]{4,3,2,1,0:T(8,128)(2,1)}), bf16[4,2,8,32,1536]{4,3,2,1,0:T(8,128)(2,1)}, u32[]{:S(2)}, u32[]{:S(2)}) async-start(bf16[4,2,8,32,1536]{4,3,2,1,0:T(8,128)(2,1)} %maximum_bitcast_fusion), calls=%async_computation.3 | async-start | bytes 12582912 | tf_op jit(solution)/shard_map/all_to_all | solution.py:206
  247.9 152.6 %reduce-scatter.5.cloned.1.call-start = ((), (), s32[]{:S(2)}) async-start(), calls=%async_computation.7 | async-start | bytes 7077888 | tf_op jit(solution)/shard_map/reduce_scatter | solution.py:226
  330.5 70.0 %copy-start.3 = (bf16[128,1536]{1,0:T(8,128)(2,1)S(1)}, bf16[128,1536]{1,0:T(8,128)(2,1)}, u32[]{:S(2)}) copy-start(bf16[128,1536]{1,0:T(8,128)(2,1)} %reduce-scatter.3.cloned.1.call-done) | copy-start | bytes 1179652
  330.6 71.3 %copy-start.27 = (f32[1536]{0:T(1024)S(1)}, f32[1536]{0:T(1024)}, u32[]{:S(2)}) copy-start(f32[1536]{0:T(1024)} %param.16) | copy-start | bytes 18436
  330.6 72.2 %copy-start.1 = (bf16[384,1536]{1,0:T(8,128)(2,1)S(1)}, bf16[384,1536]{1,0:T(8,128)(2,1)}, u32[]{:S(2)}) copy-start(bf16[384,1536]{1,0:T(8,128)(2,1)} %param.13) | copy-start | bytes 3538948
  (14 other events, 26.4 us)
Sparse Core Ops, SparseCore 0:
  11.7 33.8 reduce-scatter.2
  48.9 38.7 all-gather.1
  330.7 69.7 reduce-scatter.4
